TPU v7x, 32 devices: a whole 2x2x4 slice. The times are simulated.
32 devices in a mesh: pipe: 8 (over z, y), tensor: 4 (over x, core).
Axes of the slice: x: 2, y: 2, z: 4, core: 2. Of those that a mesh axis runs over, the one named last changes fastest.
Arguments:
- arriving: float32 [8, 8192, 384], P('pipe', 'tensor'), may hold values from -6 to 6
- stash: bfloat16 [2, 8, 8192, 384], P(None, 'pipe', 'tensor'), may hold values from -6 to 6
- grad_in: float32 [8, 8192, 384], P('pipe', 'tensor'), may hold values from -6 to 6
- first_up: bfloat16 [8, 64, 128, 128], P('pipe', 'tensor'), may hold values from -0.5 to 0.5
- second_up: bfloat16 [8, 128, 64, 256], P('pipe', 'tensor'), may hold values from -0.75 to 0.75
- first_down: bfloat16 [8, 128, 64, 256], P('pipe', 'tensor'), may hold values from -0.375 to 0.375
- second_down: bfloat16 [8, 64, 128, 128], P('pipe', 'tensor'), may hold values from -0.5 to 0.5
Outputs:
- arriving_out: float32 [8, 8192, 384], P('pipe', 'tensor')
- grad_out: float32 [8, 8192, 384], P('pipe', 'tensor')
- first_up_grad: float32 [8, 64, 128, 128], P('pipe', 'tensor')
- second_up_grad: float32 [8, 128, 64, 256], P('pipe', 'tensor')
- first_down_grad: float32 [8, 128, 64, 256], P('pipe', 'tensor')
- second_down_grad: float32 [8, 64, 128, 128], P('pipe', 'tensor')
All inputs are finite; a program needn't handle non-finite values.
Results may differ from a plain program's by a relative error of at most 0.007.
Values may be sent and summed in bfloat16 or wider, within the bound.
No kernel may reach another device: no remote copies, remote signals or barrier semaphores. Data moves between devices by JAX's collectives and lax.ppermute only.
A program may use at most 192 MiB of HBM per device.

v0:
```python
import jax
import jax.numpy as jnp
from jax import lax
from jax.sharding import PartitionSpec as P

TICKS = 2


def shifted(value, axis, by):
    count = lax.axis_size(axis)
    return lax.ppermute(value, axis, [(i, (i + by) % count) for i in range(count)])


def smooth(values):
    return jax.nn.gelu(values, approximate=True)


def to_columns(value):
    return lax.all_to_all(value, "tensor", split_axis=1, concat_axis=0, tiled=True)


def to_rows(value):
    return lax.all_to_all(value, "tensor", split_axis=0, concat_axis=1, tiled=True)


def front(narrow_in, first_up, second_up, first_down):
    first_out = jnp.einsum(
        "njr,nji->nir", narrow_in, first_up, preferred_element_type=jnp.float32
    ).astype(jnp.bfloat16)
    spread = to_columns(first_out)
    hidden_pre = jnp.einsum("nir,inf->ifr", spread, second_up, preferred_element_type=jnp.float32)
    hidden = smooth(hidden_pre).astype(jnp.bfloat16)
    local_fold = jnp.einsum(
        "ifr,inf->nir", hidden, first_down, preferred_element_type=jnp.float32
    ).astype(jnp.bfloat16)
    folded = to_rows(local_fold)
    return (spread, hidden_pre, hidden, folded)


def backward(narrow_in, cotangent, first_up, second_up, first_down, second_down, parts):
    spread, hidden_pre, hidden, folded = parts
    narrow_grad = cotangent.astype(jnp.bfloat16).reshape(narrow_in.shape)
    grad_second_down = jnp.einsum(
        "nir,nkr->nik", folded, narrow_grad, preferred_element_type=jnp.float32
    )
    local_grad = jnp.einsum(
        "nkr,nik->nir", narrow_grad, second_down, preferred_element_type=jnp.float32
    ).astype(jnp.bfloat16)
    grad_folded = to_columns(local_grad)
    grad_first_down = jnp.einsum(
        "ifr,nir->inf", hidden, grad_folded, preferred_element_type=jnp.float32
    )
    grad_hidden = jnp.einsum(
        "nir,inf->ifr", grad_folded, first_down, preferred_element_type=jnp.float32
    )
    smooth_back = jax.vjp(smooth, hidden_pre)[1]
    grad_pre = smooth_back(grad_hidden)[0].astype(jnp.bfloat16)
    grad_second_up = jnp.einsum(
        "nir,ifr->inf", spread, grad_pre, preferred_element_type=jnp.float32
    )
    column_grad = jnp.einsum(
        "ifr,inf->nir", grad_pre, second_up, preferred_element_type=jnp.float32
    ).astype(jnp.bfloat16)
    grad_first = to_rows(column_grad)
    grad_first_up = jnp.einsum(
        "njr,nir->nji", narrow_in, grad_first, preferred_element_type=jnp.float32
    )
    grad_input = cotangent + jnp.einsum(
        "nir,nji->njr", grad_first, first_up, preferred_element_type=jnp.float32
    ).reshape(cotangent.shape)
    return (grad_input, (grad_first_up, grad_second_up, grad_first_down, grad_second_down))


def body(arriving, stash, grad_in, first_up, second_up, first_down, second_down):
    activation = arriving[0]
    cotangent = grad_in[0]
    up_first = first_up[0]
    up_second = second_up[0]
    down_first = first_down[0]
    down_second = second_down[0]
    blocks = up_first.shape[0]
    width = up_first.shape[1]
    rows = activation.shape[1]
    totals = (
        jnp.zeros(up_first.shape, jnp.float32),
        jnp.zeros(up_second.shape, jnp.float32),
        jnp.zeros(down_first.shape, jnp.float32),
        jnp.zeros(down_second.shape, jnp.float32),
    )
    for position in range(TICKS):
        stored = stash[position, 0].reshape(blocks, width, rows)
        current = activation.astype(jnp.bfloat16).reshape(blocks, width, rows)
        folded_ahead = front(current, up_first, up_second, down_first)[3]
        behind = front(stored, up_first, up_second, down_first)
        output = activation + jnp.einsum(
            "nir,nik->nkr", folded_ahead, down_second, preferred_element_type=jnp.float32
        ).reshape(activation.shape)
        grad_input, terms = backward(
            stored, cotangent, up_first, up_second, down_first, down_second, behind
        )
        activation = shifted(output, "pipe", 1)
        cotangent = shifted(grad_input, "pipe", -1)
        totals = (
            totals[0] + terms[0],
            totals[1] + terms[1],
            totals[2] + terms[2],
            totals[3] + terms[3],
        )
    return (
        activation[None],
        cotangent[None],
        totals[0][None],
        totals[1][None],
        totals[2][None],
        totals[3][None],
    )


def solution(mesh):
    placed = (
        P("pipe", "tensor", None),
        P(None, "pipe", "tensor", None),
        P("pipe", "tensor", None),
        P("pipe", "tensor", None, None),
        P("pipe", "tensor", None, None),
        P("pipe", "tensor", None, None),
        P("pipe", "tensor", None, None),
    )
    return jax.shard_map(
        body,
        mesh=mesh,
        in_specs=placed,
        out_specs=(
            P("pipe", "tensor", None),
            P("pipe", "tensor", None),
            P("pipe", "tensor", None, None),
            P("pipe", "tensor", None, None),
            P("pipe", "tensor", None, None),
            P("pipe", "tensor", None, None),
        ),
        check_vma=False,
    )
```

profile of v0, /device:TPU:0, one launch (start us, length us, event | category | flops | bytes accessed | tf_op | source)
XLA Modules:
  0.0 537.9 jit_solution(9503573835288076721)
XLA Ops:
  0.7 2.3 fusion.106
  4.7 2.1 copy.92
  6.8 4.4 all-to-all-start.5
  11.2 2.1 convert_element_type.110
  15.0 2.1 copy.89
  17.1 14.8 %all-to-all-done.5 = bf16[16,128,384]{2,0,1:T(8,128)(2,1)} async-done(((bf16[16,128,384]{2,0,1:T(8,128)(2,1)}), bf16[16,128,384]{2,0,1:T(8,128)(2,1)}, u32[]{:S(2)}, u32[]{:S(2)}) %all-to-all-start.5) | async-done | bytes 1572896 | tf_op jit(solution)/shard_map/all_to_all | solution.py:19
  31.9 4.3 all-to-all-start.4
  36.3 2.1 convert_element_type.98
  38.9 2.1 copy.75
  41.0 2.9 copy.93
  43.9 12.5 %all-to-all-done.4 = bf16[16,128,384]{2,0,1:T(8,128)(2,1)} async-done(((bf16[16,128,384]{2,0,1:T(8,128)(2,1)}), bf16[16,128,384]{2,0,1:T(8,128)(2,1)}, u32[]{:S(2)}, u32[]{:S(2)}) %all-to-all-start.4) | async-done | bytes 1572896 | tf_op jit(solution)/shard_map/all_to_all | solution.py:19
  56.4 4.6 all-to-all-start
  62.9 8.8 %fusion.34 = (bf16[32,256,384]{1,2,0:T(8,128)(2,1)}, f32[32,384,256]{2,1,0:T(8,128)}) fusion(bf16[64,32,384]{2,0,1:T(8,128)(2,1)S(1)} %bitcast.275, bf16[1,32,64,256]{3,2,1,0:T(8,128)(2,1)S(1)} %copy-done), kind=kOutput, calls=%fused_computation.45 | convolution fusion | flops 430964736 | bytes 21495808 | tf_op jit(solution)/shard_map/nir,inf->ifr/dot_general | solution.py:31
  71.7 11.6 %fusion.6 = bf16[32,256,384]{1,2,0:T(8,128)(2,1)S(1)} fusion(f32[32,384,256]{2,1,0:T(8,128)} %get-tuple-element.27, bf16[64,32,384]{2,0,1:T(8,128)(2,1)S(1)} %bitcast.272, bf16[1,32,64,256]{3,2,1,0:T(8,128)(2,1)S(1)} %copy-done.28), kind=kOutput, calls=%fused_computation.12 | convolution fusion | flops 465567744 | bytes 21495808 | tf_op jit(solution)/shard_map/nir,inf->ifr/dot_general | solution.py:53
  86.0 2.1 copy.95
  88.1 4.4 all-to-all-start.6
  93.1 2.1 copy.102
  95.1 2.8 copy.76
  98.0 14.6 %all-to-all-done.6 = bf16[64,32,384]{2,1,0:T(8,128)(2,1)} async-done(((bf16[64,32,384]{2,1,0:T(8,128)(2,1)}), bf16[64,32,384]{2,1,0:T(8,128)(2,1)}, u32[]{:S(2)}, u32[]{:S(2)}) %all-to-all-start.6) | async-done | bytes 1572896 | tf_op jit(solution)/shard_map/all_to_all | solution.py:23
  112.6 4.4 all-to-all-start.8
  123.0 5.8 %collective-permute-start.2 = (f32[2048,384]{1,0:T(8,128)}, f32[2048,384]{1,0:T(8,128)}, u32[]{:S(2)}, u32[]{:S(2)}) collective-permute-start(f32[2048,384]{1,0:T(8,128)} %bitcast_add_fusion.1), channel_id=1, source_target_pairs={{0,28},{4,0},{8,4},{12,8},{16,12},{20,16},{24,20},{28,24},{1,29},{... | collective-permute-start | bytes 9437192 | tf_op jit(solution)/shard_map/ppermute | solution.py:11
  128.9 7.6 %fusion.55 = bf16[64,32,384]{2,0,1:T(8,128)(2,1)} fusion(bf16[64,32,384]{2,0,1:T(8,128)(2,1)} %bitcast.284, bf16[1,32,64,256]{3,2,1,0:T(8,128)(2,1)} %param.12, bf16[1,32,64,256]{3,2,1,0:T(8,128)(2,1)S(1)} %copy-done), kind=kOutput, calls=%fused_computation.73 | convolution fusion | flops 834404352 | bytes 5242880 | tf_op jit(solution)/shard_map/ifr,inf->nir/dot_general | solution.py:33
  136.5 3.5 copy.78
  140.0 4.4 all-to-all-start.1
  144.3 2.9 copy.103
  147.3 4.8 fusion.60
  152.1 2.1 copy.112
  154.2 10.3 %all-to-all-done.1 = bf16[64,32,384]{2,1,0:T(8,128)(2,1)} async-done(((bf16[64,32,384]{2,1,0:T(8,128)(2,1)}), bf16[64,32,384]{2,1,0:T(8,128)(2,1)}, u32[]{:S(2)}, u32[]{:S(2)}) %all-to-all-start.1) | async-done | bytes 1572896 | tf_op jit(solution)/shard_map/all_to_all | solution.py:23
  164.5 4.4 all-to-all-start.10
  174.6 6.4 %fusion.73 = f32[32,384,256]{2,1,0:T(8,128)} fusion(bf16[64,32,384]{2,0,1:T(8,128)(2,1)S(1)} %bitcast.268, bf16[1,32,64,256]{3,2,1,0:T(8,128)(2,1)S(1)} %copy-done), kind=kOutput, calls=%fused_computation.91 | convolution fusion | flops 402653184 | bytes 15204352 | tf_op jit(solution)/shard_map/nir,inf->ifr/dot_general | solution.py:31
  181.0 81.2 %collective-permute-done.2 = f32[2048,384]{1,0:T(8,128)} collective-permute-done((f32[2048,384]{1,0:T(8,128)}, f32[2048,384]{1,0:T(8,128)}, u32[]{:S(2)}, u32[]{:S(2)}) %collective-permute-start.2) | collective-permute-done | bytes 3145760 | tf_op jit(solution)/shard_map/ppermute | solution.py:11
  262.3 2.1 convert_element_type.117
  267.3 2.9 copy.98
  270.2 4.3 all-to-all-start.7
  274.5 9.1 %fusion.61 = bf16[64,32,384]{2,0,1:T(8,128)(2,1)S(1)} fusion(bf16[1,32,64,256]{3,2,1,0:T(8,128)(2,1)} %param.12, f32[32,384,256]{2,1,0:T(8,128)} %fusion.73), kind=kOutput, calls=%fused_computation.77 | convolution fusion | flops 431751168 | bytes 15204352 | tf_op jit(solution)/shard_map/ifr,inf->nir/dot_general | solution.py:33
  283.6 2.1 copy.115
  285.7 9.0 %all-to-all-done.7 = bf16[16,128,384]{2,0,1:T(8,128)(2,1)} async-done(((bf16[16,128,384]{2,0,1:T(8,128)(2,1)}), bf16[16,128,384]{2,0,1:T(8,128)(2,1)}, u32[]{:S(2)}, u32[]{:S(2)}) %all-to-all-start.7) | async-done | bytes 1572896 | tf_op jit(solution)/shard_map/all_to_all | solution.py:19
  294.7 4.4 all-to-all-start.11
  299.0 2.1 convert_element_type.104
  302.9 2.9 copy.82
  305.8 2.8 copy.100
  308.6 10.5 %all-to-all-done.11 = bf16[64,32,384]{2,1,0:T(8,128)(2,1)} async-done(((bf16[64,32,384]{2,1,0:T(8,128)(2,1)}), bf16[64,32,384]{2,1,0:T(8,128)(2,1)}, u32[]{:S(2)}, u32[]{:S(2)}) %all-to-all-start.11) | async-done | bytes 1572896 | tf_op jit(solution)/shard_map/all_to_all | solution.py:23
  319.2 4.6 all-to-all-start.2
  323.7 13.3 %fusion.13 = bf16[32,256,384]{1,2,0:T(8,128)(2,1)S(1)} fusion(f32[32,384,256]{2,1,0:T(8,128)} %fusion.73, bf16[64,32,384]{2,0,1:T(8,128)(2,1)} %bitcast.282, bf16[1,32,64,256]{3,2,1,0:T(8,128)(2,1)} %param.12), kind=kOutput, calls=%fused_computation.19 | convolution fusion | flops 465567744 | bytes 21495808 | tf_op jit(solution)/shard_map/nir,inf->ifr/dot_general | solution.py:53
  339.7 2.1 copy.105
  341.8 2.1 all-to-all-done.2
  343.9 4.6 all-to-all-start.9
  348.5 5.8 %fusion.108 = f32[32,64,256]{2,1,0:T(8,128)} fusion(bf16[64,32,384]{2,0,1:T(8,128)(2,1)} %bitcast.274, bf16[32,256,384]{1,2,0:T(8,128)(2,1)} %copy-done.1), kind=kOutput, calls=%fused_computation.122 | convolution fusion | flops 402653184 | bytes 9961472 | tf_op jit(solution)/shard_map/nir,ifr->inf/dot_general | solution.py:58
  354.3 2.8 copy.84
  357.1 7.6 %fusion.52 = bf16[64,32,384]{2,0,1:T(8,128)(2,1)} fusion(bf16[64,32,384]{2,0,1:T(8,128)(2,1)} %bitcast.285, bf16[1,32,64,256]{3,2,1,0:T(8,128)(2,1)} %param.12, bf16[1,32,64,256]{3,2,1,0:T(8,128)(2,1)S(1)} %copy-done), kind=kOutput, calls=%fused_computation.72 | convolution fusion | flops 834404352 | bytes 5242880 | tf_op jit(solution)/shard_map/ifr,inf->nir/dot_general | solution.py:33
  364.8 3.5 copy.86
  368.6 4.3 all-to-all-start.3
  373.0 5.8 %fusion.109 = f32[32,64,256]{2,1,0:T(8,128)} fusion(bf16[64,32,384]{2,0,1:T(8,128)(2,1)} %bitcast.273, bf16[32,256,384]{1,2,0:T(8,128)(2,1)} %get-tuple-element.26), kind=kOutput, calls=%fused_computation.123 | convolution fusion | flops 402653184 | bytes 9961472 | tf_op jit(solution)/shard_map/ifr,nir->inf/dot_general | solution.py:50
  378.8 2.9 copy.113
  381.7 2.8 copy.116
  387.8 3.9 bitcast_add_fusion
  391.7 2.8 collective-permute-start.3
  396.8 4.0 bitcast_add_fusion.2
  406.2 2.6 add_bitcast_fusion.1
  408.8 9.4 %add_bitcast_fusion = f32[1,32,64,256]{3,2,1,0:T(8,128)} fusion(f32[32,64,256]{2,1,0:T(8,128)S(1)} %copy-done.26, bf16[64,32,384]{2,0,1:T(8,128)(2,1)S(1)} %bitcast.283, f32[32,384,256]{2,1,0:T(8,128)} %fusion.73), kind=kOutput, calls=%fused_computation.58 | convolution fusion | flops 431489024 | bytes 18350080 | tf_op jit(solution)/shard_map/ifr,nir->inf/dot_general | solution.py:50
  420.1 2.5 copy.117
  422.6 107.2 %collective-permute-done.3 = f32[2048,384]{1,0:T(8,128)} collective-permute-done((f32[2048,384]{1,0:T(8,128)}, f32[2048,384]{1,0:T(8,128)}, u32[]{:S(2)}, u32[]{:S(2)}) %collective-permute-start.3) | collective-permute-done | bytes 3145760 | tf_op jit(solution)/shard_map/ppermute | solution.py:11
  529.9 3.8 copy.139
  533.6 3.8 copy.140
  (97 shorter events, 41.6 us)
Async XLA Ops:
  0.6 62.2 %copy-start = (bf16[1,32,64,256]{3,2,1,0:T(8,128)(2,1)S(1)}, bf16[1,32,64,256]{3,2,1,0:T(8,128)(2,1)}, u32[]{:S(2)}) copy-start(bf16[1,32,64,256]{3,2,1,0:T(8,128)(2,1)} %param.11) | copy-start | bytes 3145732
  0.6 3.5 copy-start.3
  3.0 1.1 copy-start.4
  6.8 25.1 %all-to-all-start.5 = ((bf16[16,128,384]{2,0,1:T(8,128)(2,1)}), bf16[16,128,384]{2,0,1:T(8,128)(2,1)}, u32[]{:S(2)}, u32[]{:S(2)}) async-start(bf16[16,128,384]{2,0,1:T(8,128)(2,1)} %copy.92), calls=%async_computation.5 | async-start | bytes 3145728 | tf_op jit(solution)/shard_map/all_to_all | solution.py:19
  11.2 3.3 copy-start.18
  13.3 1.1 copy-start.6
  31.9 24.5 %all-to-all-start.4 = ((bf16[16,128,384]{2,0,1:T(8,128)(2,1)}), bf16[16,128,384]{2,0,1:T(8,128)(2,1)}, u32[]{:S(2)}, u32[]{:S(2)}) async-start(bf16[16,128,384]{2,0,1:T(8,128)(2,1)} %copy.89), calls=%async_computation.4 | async-start | bytes 3145728 | tf_op jit(solution)/shard_map/all_to_all | solution.py:19
  56.4 31.7 %all-to-all-start = ((bf16[16,128,384]{2,0,1:T(8,128)(2,1)}), bf16[16,128,384]{2,0,1:T(8,128)(2,1)}, u32[]{:S(2)}, u32[]{:S(2)}) async-start(bf16[16,128,384]{2,0,1:T(8,128)(2,1)} %copy.75), calls=%async_computation | async-start | bytes 3145728 | tf_op jit(solution)/shard_map/all_to_all | solution.py:19
  61.0 1.9 copy-start.23
  62.8 8.9 %copy-start.22 = (bf16[16,4,32,384]{3,0,1,2:T(8,128)(2,1)}, bf16[16,4,32,384]{3,0,1,2:T(8,128)(2,1)S(1)}, u32[]{:S(2)}) copy-start(bf16[16,4,32,384]{3,0,1,2:T(8,128)(2,1)S(1)} %copy.90) | copy-start | bytes 4718596
  62.9 8.8 %copy-start.28 = (bf16[1,32,64,256]{3,2,1,0:T(8,128)(2,1)S(1)}, bf16[1,32,64,256]{3,2,1,0:T(8,128)(2,1)}, u32[]{:S(2)}) copy-start(bf16[1,32,64,256]{3,2,1,0:T(8,128)(2,1)} %param.12) | copy-start | bytes 3145732
  83.3 2.7 copy-start.1
  88.1 24.5 %all-to-all-start.6 = ((bf16[64,32,384]{2,1,0:T(8,128)(2,1)}), bf16[64,32,384]{2,1,0:T(8,128)(2,1)}, u32[]{:S(2)}, u32[]{:S(2)}) async-start(bf16[64,32,384]{2,1,0:T(8,128)(2,1)} %copy.95), calls=%async_computation.6 | async-start | bytes 3145728 | tf_op jit(solution)/shard_map/all_to_all | solution.py:23
  112.6 27.4 %all-to-all-start.8 = ((bf16[16,128,384]{2,0,1:T(8,128)(2,1)}), bf16[16,128,384]{2,0,1:T(8,128)(2,1)}, u32[]{:S(2)}, u32[]{:S(2)}) async-start(bf16[16,128,384]{2,0,1:T(8,128)(2,1)} %copy.102), calls=%async_computation.8 | async-start | bytes 3145728 | tf_op jit(solution)/shard_map/all_to_all | solution.py:19
  118.6 1.2 copy-start.10
  118.6 2.5 copy-start.16
  123.0 139.2 %collective-permute-start.2 = (f32[2048,384]{1,0:T(8,128)}, f32[2048,384]{1,0:T(8,128)}, u32[]{:S(2)}, u32[]{:S(2)}) collective-permute-start(f32[2048,384]{1,0:T(8,128)} %bitcast_add_fusion.1), channel_id=1, source_target_pairs={{0,28},{4,0},{8,4},{12,8},{16,12},{20,16},{24,20},{28,24},{1,29},{... | collective-permute-start | bytes 9437192 | tf_op jit(solution)/shard_map/ppermute | solution.py:11
  140.0 24.5 %all-to-all-start.1 = ((bf16[64,32,384]{2,1,0:T(8,128)(2,1)}), bf16[64,32,384]{2,1,0:T(8,128)(2,1)}, u32[]{:S(2)}, u32[]{:S(2)}) async-start(bf16[64,32,384]{2,1,0:T(8,128)(2,1)} %copy.78), calls=%async_computation.1 | async-start | bytes 3145728 | tf_op jit(solution)/shard_map/all_to_all | solution.py:23
  144.3 2.9 copy-start.29
  164.5 105.7 %all-to-all-start.10 = ((bf16[64,32,384]{2,1,0:T(8,128)(2,1)}), bf16[64,32,384]{2,1,0:T(8,128)(2,1)}, u32[]{:S(2)}, u32[]{:S(2)}) async-start(bf16[64,32,384]{2,1,0:T(8,128)(2,1)} %copy.112), calls=%async_computation.10 | async-start | bytes 3145728 | tf_op jit(solution)/shard_map/all_to_all | solution.py:23
  168.8 1.8 copy-start.19
  170.6 1.9 copy-start.17
  172.5 2.1 copy-start.12
  174.4 124.6 %collective-permute-start = (f32[2048,384]{1,0:T(8,128)}, f32[2048,384]{1,0:T(8,128)}, u32[]{:S(2)}, u32[]{:S(2)}) collective-permute-start(f32[2048,384]{1,0:T(8,128)} %bitcast_add_fusion.3), channel_id=1, source_target_pairs={{0,4},{4,8},{8,12},{12,16},{16,20},{20,24},{24,28},{28,0},{1,5},{5... | collective-permute-start | bytes 9437192 | tf_op jit(solution)/shard_map/ppermute | solution.py:11
  264.3 1.2 copy-start.8
  270.2 24.5 %all-to-all-start.7 = ((bf16[16,128,384]{2,0,1:T(8,128)(2,1)}), bf16[16,128,384]{2,0,1:T(8,128)(2,1)}, u32[]{:S(2)}, u32[]{:S(2)}) async-start(bf16[16,128,384]{2,0,1:T(8,128)(2,1)} %copy.98), calls=%async_computation.7 | async-start | bytes 3145728 | tf_op jit(solution)/shard_map/all_to_all | solution.py:19
  294.7 24.5 %all-to-all-start.11 = ((bf16[64,32,384]{2,1,0:T(8,128)(2,1)}), bf16[64,32,384]{2,1,0:T(8,128)(2,1)}, u32[]{:S(2)}, u32[]{:S(2)}) async-start(bf16[64,32,384]{2,1,0:T(8,128)(2,1)} %copy.115), calls=%async_computation.11 | async-start | bytes 3145728 | tf_op jit(solution)/shard_map/all_to_all | solution.py:23
  319.2 24.7 %all-to-all-start.2 = ((bf16[16,128,384]{2,0,1:T(8,128)(2,1)}), bf16[16,128,384]{2,0,1:T(8,128)(2,1)}, u32[]{:S(2)}, u32[]{:S(2)}) async-start(bf16[16,128,384]{2,0,1:T(8,128)(2,1)} %copy.82), calls=%async_computation.2 | async-start | bytes 3145728 | tf_op jit(solution)/shard_map/all_to_all | solution.py:19
  337.0 2.7 copy-start.2
  343.9 24.7 %all-to-all-start.9 = ((bf16[64,32,384]{2,1,0:T(8,128)(2,1)}), bf16[64,32,384]{2,1,0:T(8,128)(2,1)}, u32[]{:S(2)}, u32[]{:S(2)}) async-start(bf16[64,32,384]{2,1,0:T(8,128)(2,1)} %copy.105), calls=%async_computation.9 | async-start | bytes 3145728 | tf_op jit(solution)/shard_map/all_to_all | solution.py:23
  368.6 25.9 %all-to-all-start.3 = ((bf16[64,32,384]{2,1,0:T(8,128)(2,1)}), bf16[64,32,384]{2,1,0:T(8,128)(2,1)}, u32[]{:S(2)}, u32[]{:S(2)}) async-start(bf16[64,32,384]{2,1,0:T(8,128)(2,1)} %copy.86), calls=%async_computation.3 | async-start | bytes 3145728 | tf_op jit(solution)/shard_map/all_to_all | solution.py:23
  386.1 1.1 copy-start.14
  391.7 4.5 copy-start.20
  391.7 138.2 %collective-permute-start.3 = (f32[2048,384]{1,0:T(8,128)}, f32[2048,384]{1,0:T(8,128)}, u32[]{:S(2)}, u32[]{:S(2)}) collective-permute-start(f32[2048,384]{1,0:T(8,128)} %bitcast_add_fusion), channel_id=1, source_target_pairs={{0,28},{4,0},{8,4},{12,8},{16,12},{20,16},{24,20},{28,24},{1,29},{... | collective-permute-start | bytes 9437192 | tf_op jit(solution)/shard_map/ppermute | solution.py:11
  396.8 4.3 copy-start.5
  396.8 4.3 copy-start.11
  396.8 5.1 copy-start.25
  396.8 6.2 %copy-start.24 = (bf16[4,16,32,384]{3,2,0,1:T(8,128)(2,1)S(1)}, bf16[4,16,32,384]{3,2,0,1:T(8,128)(2,1)}, u32[]{:S(2)}) copy-start(bf16[4,16,32,384]{3,2,0,1:T(8,128)(2,1)} %copy.116) | copy-start | bytes 4718596
  400.8 1.4 copy-start.7
  400.8 129.0 %collective-permute-start.1 = (f32[2048,384]{1,0:T(8,128)}, f32[2048,384]{1,0:T(8,128)}, u32[]{:S(2)}, u32[]{:S(2)}) collective-permute-start(f32[2048,384]{1,0:T(8,128)} %bitcast_add_fusion.2), channel_id=1, source_target_pairs={{0,4},{4,8},{8,12},{12,16},{16,20},{20,24},{24,28},{28,0},{1,5},{5... | collective-permute-start | bytes 9437192 | tf_op jit(solution)/shard_map/ppermute | solution.py:11
  401.2 4.3 slice-start
  401.9 1.8 copy-start.9
  402.3 3.2 slice-start.1
  403.0 2.4 copy-start.13
  403.1 3.2 copy-start.21
  406.2 2.6 copy-start.26
  406.2 2.6 copy-start.27
  408.8 9.4 %copy-start.15 = (bf16[4,16,32,384]{3,2,0,1:T(8,128)(2,1)S(1)}, bf16[4,16,32,384]{3,2,0,1:T(8,128)(2,1)}, u32[]{:S(2)}) copy-start(bf16[4,16,32,384]{3,2,0,1:T(8,128)(2,1)} %copy-done.14) | copy-start | bytes 4718596
where the time goes:
time: 545 us; the launch traced here: 538 us
  waiting for transfers between devices  263 us (48%)
  matrix products  111 us (20%)
  local copies, waits for them, and re-layouts  80.8 us (15%)
  starting transfers between devices  62 us (11%)
  other arithmetic  20.1 us (4%)
    ppermute x4, waiting for transfers between devices, shifted(): lax.ppermute(value, axis, [(i, (i + by) % count) for i in range(count)])  188 us
    all_to_all x6, waiting for transfers between devices, to_columns(): lax.all_to_all(value, 'tensor', split_axis=1, concat_axis=0, tiled=True)  38.4 us
    all_to_all x6, waiting for transfers between devices, to_rows(): lax.all_to_all(value, 'tensor', split_axis=0, concat_axis=1, tiled=True)  35.8 us
    dot_general x4, matrix products, front(): jnp.einsum('ifr,inf->nir', hidden, first_down, preferred_element_type=jnp...  29.2 us
    all_to_all x6, starting transfers between devices, to_columns(): lax.all_to_all(value, 'tensor', split_axis=1, concat_axis=0, tiled=True)  26.6 us
    all_to_all x6, starting transfers between devices, to_rows(): lax.all_to_all(value, 'tensor', split_axis=0, concat_axis=1, tiled=True)  26.4 us
    dot_general x2, matrix products, backward(): jnp.einsum('nir,inf->ifr', grad_folded, first_down, preferred_element_typ...  24.9 us
    unnamed x67, local copies, waits for them, and re-layouts  20.8 us
  transfers between devices with their start and end apart: 16, of which 10 were waited for; matrix products, arithmetic and copies ran while one was open for 35% of the time, Pallas kernels for 0%

commit v1 on v0

--- a/solution.py
+++ b/solution.py
@@ -2,8 +2,6 @@
 import jax.numpy as jnp
 from jax import lax
 from jax.sharding import PartitionSpec as P
-
-TICKS = 2
 
 
 def shifted(value, axis, by):
@@ -65,7 +63,7 @@
     grad_first_up = jnp.einsum(
         "njr,nir->nji", narrow_in, grad_first, preferred_element_type=jnp.float32
     )
-    grad_input = cotangent + jnp.einsum(
+    grad_input = jnp.einsum(
         "nir,nji->njr", grad_first, first_up, preferred_element_type=jnp.float32
     ).reshape(cotangent.shape)
     return (grad_input, (grad_first_up, grad_second_up, grad_first_down, grad_second_down))
@@ -81,31 +79,41 @@
     blocks = up_first.shape[0]
     width = up_first.shape[1]
     rows = activation.shape[1]
+    stored = stash[0, 0].reshape(blocks, width, rows)
+    current = activation.astype(jnp.bfloat16).reshape(blocks, width, rows)
+    folded_ahead = front(current, up_first, up_second, down_first)[3]
+    behind = front(stored, up_first, up_second, down_first)
+    output = activation + jnp.einsum(
+        "nir,nik->nkr", folded_ahead, down_second, preferred_element_type=jnp.float32
+    ).reshape(activation.shape)
+    grad_input, terms = backward(
+        stored, cotangent, up_first, up_second, down_first, down_second, behind
+    )
+    grad_input = cotangent + grad_input
+    totals = terms
+    near_activation = shifted(output.astype(jnp.bfloat16), "pipe", 1)
+    near_cotangent = shifted(grad_input.astype(jnp.bfloat16), "pipe", -1)
+    far_activation = shifted(output, "pipe", 2)
+    far_cotangent = shifted(grad_input, "pipe", -2)
+
+    stored = stash[1, 0].reshape(blocks, width, rows)
+    current = near_activation.reshape(blocks, width, rows)
+    folded_ahead = front(current, up_first, up_second, down_first)[3]
+    behind = front(stored, up_first, up_second, down_first)
+    step = jnp.einsum(
+        "nir,nik->nkr", folded_ahead, down_second, preferred_element_type=jnp.float32
+    ).reshape(activation.shape)
+    grad_step, terms = backward(
+        stored, near_cotangent, up_first, up_second, down_first, down_second, behind
+    )
+    activation = far_activation + shifted(step.astype(jnp.bfloat16), "pipe", 1)
+    cotangent = far_cotangent + shifted(grad_step.astype(jnp.bfloat16), "pipe", -1)
     totals = (
-        jnp.zeros(up_first.shape, jnp.float32),
-        jnp.zeros(up_second.shape, jnp.float32),
-        jnp.zeros(down_first.shape, jnp.float32),
-        jnp.zeros(down_second.shape, jnp.float32),
+        totals[0] + terms[0],
+        totals[1] + terms[1],
+        totals[2] + terms[2],
+        totals[3] + terms[3],
     )
-    for position in range(TICKS):
-        stored = stash[position, 0].reshape(blocks, width, rows)
-        current = activation.astype(jnp.bfloat16).reshape(blocks, width, rows)
-        folded_ahead = front(current, up_first, up_second, down_first)[3]
-        behind = front(stored, up_first, up_second, down_first)
-        output = activation + jnp.einsum(
-            "nir,nik->nkr", folded_ahead, down_second, preferred_element_type=jnp.float32
-        ).reshape(activation.shape)
-        grad_input, terms = backward(
-            stored, cotangent, up_first, up_second, down_first, down_second, behind
-        )
-        activation = shifted(output, "pipe", 1)
-        cotangent = shifted(grad_input, "pipe", -1)
-        totals = (
-            totals[0] + terms[0],
-            totals[1] + terms[1],
-            totals[2] + terms[2],
-            totals[3] + terms[3],
-        )
     return (
         activation[None],
         cotangent[None],

time: 545 us -> 496 us (0.910)
  waiting for transfers between devices: 263 us -> 222 us
  local copies, waits for them, and re-layouts: 80.8 us -> 64.9 us
  starting transfers between devices: 62 us -> 67.6 us
    ppermute x4 -> x6, waiting for transfers between devices: 188 us -> 151 us  [shifted(): lax.ppermute(value, axis, [(i, (i + by) % count) for i in range(count)])]
    all_to_all x6, waiting for transfers between devices: 35.8 us -> 16.7 us  [to_rows(): lax.all_to_all(value, 'tensor', split_axis=0, concat_axis=1, tiled=True)]
    all_to_all x6, waiting for transfers between devices: 38.4 us -> 53.8 us  [to_columns(): lax.all_to_all(value, 'tensor', split_axis=1, concat_axis=0, tiled=True)]
    add x4 -> x0, other arithmetic: 11.8 us -> none  [the longest x2 5.97 us: body(): activation + jnp.einsum('nir,nik->nkr', folded_ahead, down_second, prefer...]
    unnamed x67 -> x69, local copies, waits for them, and re-layouts: 20.8 us -> 9.86 us
    broadcast_in_dim x0 -> x2, other arithmetic: none -> 8.55 us  [the longest x1 4.27 us: body(): activation[None]]
    ppermute x4 -> x6, starting transfers between devices: 9.05 us -> 14.4 us  [shifted(): lax.ppermute(value, axis, [(i, (i + by) % count) for i in range(count)])]
  transfers between devices with their start and end apart: 16 -> 18, of which waited for: 10 -> 12; matrix products, arithmetic and copies ran while one was open for 35% -> 37% of each run, Pallas kernels for 0% -> 0%
where the time goes in v1:
time: 496 us; the launch traced here: 487 us
  waiting for transfers between devices  222 us (45%)
  matrix products  115 us (23%)
  starting transfers between devices  67.6 us (14%)
  local copies, waits for them, and re-layouts  64.9 us (13%)
  other arithmetic  16.1 us (3%)
    ppermute x6, waiting for transfers between devices, shifted(): lax.ppermute(value, axis, [(i, (i + by) % count) for i in range(count)])  151 us
    all_to_all x6, waiting for transfers between devices, to_columns(): lax.all_to_all(value, 'tensor', split_axis=1, concat_axis=0, tiled=True)  53.8 us
    dot_general x4, matrix products, front(): jnp.einsum('ifr,inf->nir', hidden, first_down, preferred_element_type=jnp...  27.5 us
    all_to_all x6, starting transfers between devices, to_rows(): lax.all_to_all(value, 'tensor', split_axis=0, concat_axis=1, tiled=True)  26.7 us
    all_to_all x6, starting transfers between devices, to_columns(): lax.all_to_all(value, 'tensor', split_axis=1, concat_axis=0, tiled=True)  26.5 us
    dot_general x2, matrix products, backward(): jnp.einsum('nir,inf->ifr', grad_folded, first_down, preferred_element_typ...  23.9 us
    all_to_all x6, waiting for transfers between devices, to_rows(): lax.all_to_all(value, 'tensor', split_axis=0, concat_axis=1, tiled=True)  16.7 us
    dot_general x2, matrix products, front(): jnp.einsum('nir,inf->ifr', spread, second_up, preferred_element_type=jnp....  15.2 us
  transfers between devices with their start and end apart: 18, of which 12 were waited for; matrix products, arithmetic and copies ran while one was open for 37% of the time, Pallas kernels for 0%

profile of v1, /device:TPU:0, one launch (start us, length us, event | category | flops | bytes accessed | tf_op | source)
XLA Modules:
  0.0 486.7 jit_solution(14752777507703864372)
XLA Ops:
  0.7 2.3 fusion.106
  4.8 2.1 copy.92
  6.8 4.4 all-to-all-start.5
  11.2 2.1 convert_element_type.138
  15.1 2.1 copy.89
  17.1 14.8 %all-to-all-done.5 = bf16[16,128,384]{2,0,1:T(8,128)(2,1)} async-done(((bf16[16,128,384]{2,0,1:T(8,128)(2,1)}), bf16[16,128,384]{2,0,1:T(8,128)(2,1)}, u32[]{:S(2)}, u32[]{:S(2)}) %all-to-all-start.5) | async-done | bytes 1572896 | tf_op jit(solution)/shard_map/all_to_all | solution.py:17
  31.9 4.3 all-to-all-start.4
  36.9 2.1 copy.102
  39.2 17.3 %all-to-all-done.4 = bf16[16,128,384]{2,0,1:T(8,128)(2,1)} async-done(((bf16[16,128,384]{2,0,1:T(8,128)(2,1)}), bf16[16,128,384]{2,0,1:T(8,128)(2,1)}, u32[]{:S(2)}, u32[]{:S(2)}) %all-to-all-start.4) | async-done | bytes 1572896 | tf_op jit(solution)/shard_map/all_to_all | solution.py:17
  56.4 4.4 all-to-all-start.8
  61.4 2.1 copy.75
  65.2 2.3 copy.90
  67.5 8.8 %fusion.34 = (bf16[32,256,384]{1,2,0:T(8,128)(2,1)}, f32[32,384,256]{2,1,0:T(8,128)}) fusion(bf16[64,32,384]{2,0,1:T(8,128)(2,1)S(1)} %bitcast.276, bf16[1,32,64,256]{3,2,1,0:T(8,128)(2,1)S(1)} %copy-done), kind=kOutput, calls=%fused_computation.45 | convolution fusion | flops 430964736 | bytes 21495808 | tf_op jit(solution)/shard_map/nir,inf->ifr/dot_general | solution.py:29
  76.2 4.7 all-to-all-done.8
  80.9 4.5 all-to-all-start
  85.5 11.9 %fusion.6 = bf16[32,256,384]{1,2,0:T(8,128)(2,1)S(1)} fusion(f32[32,384,256]{2,1,0:T(8,128)} %get-tuple-element.31, bf16[64,32,384]{2,0,1:T(8,128)(2,1)S(1)} %bitcast.274, bf16[1,32,64,256]{3,2,1,0:T(8,128)(2,1)} %param.12), kind=kOutput, calls=%fused_computation.12 | convolution fusion | flops 465567744 | bytes 21495808 | tf_op jit(solution)/shard_map/nir,inf->ifr/dot_general | solution.py:51
  100.1 2.1 copy.95
  102.1 3.4 all-to-all-done
  105.6 4.3 all-to-all-start.6
  109.9 4.8 fusion.60
  116.5 2.1 copy.112
  118.5 2.8 copy.76
  121.4 7.6 %fusion.55 = bf16[64,32,384]{2,0,1:T(8,128)(2,1)} fusion(bf16[64,32,384]{2,0,1:T(8,128)(2,1)} %bitcast.285, bf16[1,32,64,256]{3,2,1,0:T(8,128)(2,1)} %param.12, bf16[1,32,64,256]{3,2,1,0:T(8,128)(2,1)S(1)} %copy-done), kind=kOutput, calls=%fused_computation.75 | convolution fusion | flops 834404352 | bytes 5242880 | tf_op jit(solution)/shard_map/ifr,inf->nir/dot_general | solution.py:31
  129.0 3.5 copy.78
  132.5 4.4 all-to-all-start.1
  141.0 2.6 fusion.104
  143.6 5.4 %collective-permute-start.4 = (bf16[2048,384]{1,0:T(8,128)(2,1)}, bf16[2048,384]{1,0:T(8,128)(2,1)}, u32[]{:S(2)}, u32[]{:S(2)}) collective-permute-start(bf16[2048,384]{1,0:T(8,128)(2,1)} %get-tuple-element.24), channel_id=1, source_target_pairs={{0,28},{4,0},{8,4},{12,8},{16,12},{20,16},{24,20},{28,24},{1,29},{... | collective-permute-start | bytes 4718600 | tf_op jit(solution)/shard_map/ppermute | solution.py:9
  149.0 6.4 %fusion.73 = f32[32,384,256]{2,1,0:T(8,128)} fusion(bf16[64,32,384]{2,0,1:T(8,128)(2,1)S(1)} %bitcast.270, bf16[1,32,64,256]{3,2,1,0:T(8,128)(2,1)S(1)} %copy-done), kind=kOutput, calls=%fused_computation.93 | convolution fusion | flops 402653184 | bytes 15204352 | tf_op jit(solution)/shard_map/nir,inf->ifr/dot_general | solution.py:29
  157.0 4.7 all-to-all-start.10
  165.3 2.6 fusion.105
  167.9 2.4 collective-permute-start.1
  170.3 44.7 %collective-permute-done.4 = bf16[2048,384]{1,0:T(8,128)(2,1)} collective-permute-done((bf16[2048,384]{1,0:T(8,128)(2,1)}, bf16[2048,384]{1,0:T(8,128)(2,1)}, u32[]{:S(2)}, u32[]{:S(2)}) %collective-permute-start.4) | collective-permute-done | bytes 1572896 | tf_op jit(solution)/shard_map/ppermute | solution.py:9
  215.0 3.2 fusion.63
  218.2 3.1 copy.98
  221.2 4.4 all-to-all-start.7
  225.6 7.9 %fusion.61 = bf16[64,32,384]{2,0,1:T(8,128)(2,1)S(1)} fusion(bf16[1,32,64,256]{3,2,1,0:T(8,128)(2,1)S(1)} %copy-done.31, f32[32,384,256]{2,1,0:T(8,128)} %fusion.73), kind=kOutput, calls=%fused_computation.79 | convolution fusion | flops 431751168 | bytes 15204352 | tf_op jit(solution)/shard_map/ifr,inf->nir/dot_general | solution.py:31
  233.6 2.1 copy.115
  235.6 10.1 %all-to-all-done.7 = bf16[16,128,384]{2,0,1:T(8,128)(2,1)} async-done(((bf16[16,128,384]{2,0,1:T(8,128)(2,1)}), bf16[16,128,384]{2,0,1:T(8,128)(2,1)}, u32[]{:S(2)}, u32[]{:S(2)}) %all-to-all-start.7) | async-done | bytes 1572896 | tf_op jit(solution)/shard_map/all_to_all | solution.py:17
  245.8 4.4 all-to-all-start.11
  250.1 5.4 %fusion.108 = f32[32,64,256]{2,1,0:T(8,128)} fusion(bf16[64,32,384]{2,0,1:T(8,128)(2,1)S(1)} %bitcast.277, bf16[32,256,384]{1,2,0:T(8,128)(2,1)} %copy-done.1), kind=kOutput, calls=%fused_computation.124 | convolution fusion | flops 402653184 | bytes 9961472 | tf_op jit(solution)/shard_map/nir,ifr->inf/dot_general | solution.py:56
  261.1 9.1 %all-to-all-done.11 = bf16[64,32,384]{2,1,0:T(8,128)(2,1)} async-done(((bf16[64,32,384]{2,1,0:T(8,128)(2,1)}), bf16[64,32,384]{2,1,0:T(8,128)(2,1)}, u32[]{:S(2)}, u32[]{:S(2)}) %all-to-all-start.11) | async-done | bytes 1572896 | tf_op jit(solution)/shard_map/all_to_all | solution.py:21
  270.3 4.5 all-to-all-start.2
  274.8 11.9 %fusion.13 = bf16[32,256,384]{1,2,0:T(8,128)(2,1)S(1)} fusion(f32[32,384,256]{2,1,0:T(8,128)} %fusion.73, bf16[64,32,384]{2,0,1:T(8,128)(2,1)S(1)} %bitcast.283, bf16[1,32,64,256]{3,2,1,0:T(8,128)(2,1)} %param.12), kind=kOutput, calls=%fused_computation.19 | convolution fusion | flops 465567744 | bytes 21495808 | tf_op jit(solution)/shard_map/nir,inf->ifr/dot_general | solution.py:51
  289.4 2.1 copy.105
  291.5 3.4 all-to-all-done.2
  294.9 4.3 all-to-all-start.9
  299.3 5.4 %fusion.109 = f32[32,64,256]{2,1,0:T(8,128)} fusion(bf16[64,32,384]{2,0,1:T(8,128)(2,1)S(1)} %bitcast.275, bf16[32,256,384]{1,2,0:T(8,128)(2,1)} %get-tuple-element.30), kind=kOutput, calls=%fused_computation.125 | convolution fusion | flops 402653184 | bytes 9961472 | tf_op jit(solution)/shard_map/ifr,nir->inf/dot_general | solution.py:48
  304.6 3.8 collective-permute-start.3
  308.5 2.8 copy.113
  311.3 2.8 copy.116
  315.8 7.1 %fusion.52 = bf16[64,32,384]{2,0,1:T(8,128)(2,1)} fusion(bf16[64,32,384]{2,0,1:T(8,128)(2,1)S(1)} %bitcast.286, bf16[1,32,64,256]{3,2,1,0:T(8,128)(2,1)} %param.12, bf16[1,32,64,256]{3,2,1,0:T(8,128)(2,1)S(1)} %copy-done), kind=kOutput, calls=%fused_computation.74 | convolution fusion | flops 834404352 | bytes 5242880 | tf_op jit(solution)/shard_map/ifr,inf->nir/dot_general | solution.py:31
  322.9 3.6 copy.86
  326.5 4.6 all-to-all-start.3
  331.1 3.3 fusion.107
  335.8 3.2 fusion.64
  342.4 2.8 collective-permute-start.5
  345.2 6.0 %all-to-all-done.3 = bf16[64,32,384]{2,1,0:T(8,128)(2,1)} async-done(((bf16[64,32,384]{2,1,0:T(8,128)(2,1)}), bf16[64,32,384]{2,1,0:T(8,128)(2,1)}, u32[]{:S(2)}, u32[]{:S(2)}) %all-to-all-start.3) | async-done | bytes 1572896 | tf_op jit(solution)/shard_map/all_to_all | solution.py:21
  354.9 9.5 %add_bitcast_fusion.2 = f32[1,32,64,256]{3,2,1,0:T(8,128)} fusion(f32[32,64,256]{2,1,0:T(8,128)S(1)} %copy-done.27, bf16[64,32,384]{2,0,1:T(8,128)(2,1)S(1)} %bitcast.284, f32[32,384,256]{2,1,0:T(8,128)} %fusion.73), kind=kOutput, calls=%fused_computation.58 | convolution fusion | flops 431489024 | bytes 18350080 | tf_op jit(solution)/shard_map/ifr,nir->inf/dot_general | solution.py:48
  364.4 2.6 add_bitcast_fusion.3
  368.8 2.5 copy.117
  371.4 5.9 %collective-permute-done.3 = f32[2048,384]{1,0:T(8,128)} collective-permute-done((f32[2048,384]{1,0:T(8,128)}, f32[2048,384]{1,0:T(8,128)}, u32[]{:S(2)}, u32[]{:S(2)}) %collective-permute-start.3) | collective-permute-done | bytes 3145760 | tf_op jit(solution)/shard_map/ppermute | solution.py:9
  377.2 100.7 %collective-permute-done.5 = bf16[2048,384]{1,0:T(8,128)(2,1)} collective-permute-done((bf16[2048,384]{1,0:T(8,128)(2,1)}, bf16[2048,384]{1,0:T(8,128)(2,1)}, u32[]{:S(2)}, u32[]{:S(2)}) %collective-permute-start.5) | collective-permute-done | bytes 1572896 | tf_op jit(solution)/shard_map/ppermute | solution.py:9
  477.9 4.3 add_bitcast_fusion
  482.2 4.3 add_bitcast_fusion.1
  (101 shorter events, 40.4 us)
Async XLA Ops:
  0.6 66.8 %copy-start = (bf16[1,32,64,256]{3,2,1,0:T(8,128)(2,1)S(1)}, bf16[1,32,64,256]{3,2,1,0:T(8,128)(2,1)}, u32[]{:S(2)}) copy-start(bf16[1,32,64,256]{3,2,1,0:T(8,128)(2,1)} %param.11) | copy-start | bytes 3145732
  0.6 3.5 copy-start.3
  3.0 1.2 copy-start.6
  3.0 33.3 %copy-start.4 = (bf16[1,1,2048,384]{3,2,1,0:T(8,128)(2,1)}, bf16[1,1,2048,384]{3,2,1,0:T(8,128)(2,1)S(1)}, u32[]{:S(2)}) copy-start(bf16[1,1,2048,384]{3,2,1,0:T(8,128)(2,1)S(1)} %get-tuple-element.28) | copy-start | bytes 4718596
  6.8 25.1 %all-to-all-start.5 = ((bf16[16,128,384]{2,0,1:T(8,128)(2,1)}), bf16[16,128,384]{2,0,1:T(8,128)(2,1)}, u32[]{:S(2)}, u32[]{:S(2)}) async-start(bf16[16,128,384]{2,0,1:T(8,128)(2,1)} %copy.92), calls=%async_computation.5 | async-start | bytes 3145728 | tf_op jit(solution)/shard_map/all_to_all | solution.py:17
  11.2 3.3 copy-start.16
  13.3 1.2 copy-start.8
  31.9 24.5 %all-to-all-start.4 = ((bf16[16,128,384]{2,0,1:T(8,128)(2,1)}), bf16[16,128,384]{2,0,1:T(8,128)(2,1)}, u32[]{:S(2)}, u32[]{:S(2)}) async-start(bf16[16,128,384]{2,0,1:T(8,128)(2,1)} %copy.89), calls=%async_computation.4 | async-start | bytes 3145728 | tf_op jit(solution)/shard_map/all_to_all | solution.py:17
  36.3 2.7 copy-start.14
  56.4 24.5 %all-to-all-start.8 = ((bf16[16,128,384]{2,0,1:T(8,128)(2,1)}), bf16[16,128,384]{2,0,1:T(8,128)(2,1)}, u32[]{:S(2)}, u32[]{:S(2)}) async-start(bf16[16,128,384]{2,0,1:T(8,128)(2,1)} %copy.102), calls=%async_computation.8 | async-start | bytes 3145728 | tf_op jit(solution)/shard_map/all_to_all | solution.py:17
  65.2 2.3 copy-start.22
  67.4 18.0 %copy-start.20 = (bf16[16,4,32,384]{3,0,1,2:T(8,128)(2,1)}, bf16[16,4,32,384]{3,0,1,2:T(8,128)(2,1)S(1)}, u32[]{:S(2)}) copy-start(bf16[16,4,32,384]{3,0,1,2:T(8,128)(2,1)S(1)} %copy.90) | copy-start | bytes 4718596
  80.9 24.7 %all-to-all-start = ((bf16[16,128,384]{2,0,1:T(8,128)(2,1)}), bf16[16,128,384]{2,0,1:T(8,128)(2,1)}, u32[]{:S(2)}, u32[]{:S(2)}) async-start(bf16[16,128,384]{2,0,1:T(8,128)(2,1)} %copy.75), calls=%async_computation | async-start | bytes 3145728 | tf_op jit(solution)/shard_map/all_to_all | solution.py:17
  97.4 2.7 copy-start.1
  100.1 9.9 %copy-start.30 = (bf16[1,32,64,256]{3,2,1,0:T(8,128)(2,1)S(1)}, bf16[1,32,64,256]{3,2,1,0:T(8,128)(2,1)}, u32[]{:S(2)}) copy-start(bf16[1,32,64,256]{3,2,1,0:T(8,128)(2,1)} %param.12) | copy-start | bytes 3145732
  105.6 26.9 %all-to-all-start.6 = ((bf16[64,32,384]{2,1,0:T(8,128)(2,1)}), bf16[64,32,384]{2,1,0:T(8,128)(2,1)}, u32[]{:S(2)}, u32[]{:S(2)}) async-start(bf16[64,32,384]{2,1,0:T(8,128)(2,1)} %copy.95), calls=%async_computation.6 | async-start | bytes 3145728 | tf_op jit(solution)/shard_map/all_to_all | solution.py:21
  116.5 32.6 %copy-start.10 = (bf16[16,4,32,384]{3,0,1,2:T(8,128)(2,1)}, bf16[16,4,32,384]{3,0,1,2:T(8,128)(2,1)S(1)}, u32[]{:S(2)}) copy-start(bf16[16,4,32,384]{3,0,1,2:T(8,128)(2,1)S(1)} %copy.103) | copy-start | bytes 4718596
  132.5 24.5 %all-to-all-start.1 = ((bf16[64,32,384]{2,1,0:T(8,128)(2,1)}), bf16[64,32,384]{2,1,0:T(8,128)(2,1)}, u32[]{:S(2)}, u32[]{:S(2)}) async-start(bf16[64,32,384]{2,1,0:T(8,128)(2,1)} %copy.78), calls=%async_computation.1 | async-start | bytes 3145728 | tf_op jit(solution)/shard_map/all_to_all | solution.py:21
  138.5 1.2 copy-start.12
  138.5 2.5 copy-start.13
  143.6 71.4 %collective-permute-start.4 = (bf16[2048,384]{1,0:T(8,128)(2,1)}, bf16[2048,384]{1,0:T(8,128)(2,1)}, u32[]{:S(2)}, u32[]{:S(2)}) collective-permute-start(bf16[2048,384]{1,0:T(8,128)(2,1)} %get-tuple-element.24), channel_id=1, source_target_pairs={{0,28},{4,0},{8,4},{12,8},{16,12},{20,16},{24,20},{28,24},{1,29},{... | collective-permute-start | bytes 4718600 | tf_op jit(solution)/shard_map/ppermute | solution.py:9
  155.4 8.0 %copy-start.17 = (bf16[1,16,128,128]{3,2,1,0:T(8,128)(2,1)S(1)}, bf16[1,16,128,128]{3,2,1,0:T(8,128)(2,1)}, u32[]{:S(2)}) copy-start(bf16[1,16,128,128]{3,2,1,0:T(8,128)(2,1)} %param.13) | copy-start | bytes 1572868
  157.0 64.3 %all-to-all-start.10 = ((bf16[64,32,384]{2,1,0:T(8,128)(2,1)}), bf16[64,32,384]{2,1,0:T(8,128)(2,1)}, u32[]{:S(2)}, u32[]{:S(2)}) async-start(bf16[64,32,384]{2,1,0:T(8,128)(2,1)} %copy.112), calls=%async_computation.10 | async-start | bytes 3145728 | tf_op jit(solution)/shard_map/all_to_all | solution.py:21
  163.4 1.9 copy-start.15
  167.9 87.6 %collective-permute-start.1 = (bf16[2048,384]{1,0:T(8,128)(2,1)}, bf16[2048,384]{1,0:T(8,128)(2,1)}, u32[]{:S(2)}, u32[]{:S(2)}) collective-permute-start(bf16[2048,384]{1,0:T(8,128)(2,1)} %get-tuple-element.26), channel_id=1, source_target_pairs={{0,4},{4,8},{8,12},{12,16},{16,20},{20,24},{24,28},{28,0},{1,5},{5... | collective-permute-start | bytes 4718600 | tf_op jit(solution)/shard_map/ppermute | solution.py:9
  218.2 7.4 %copy-start.31 = (bf16[1,32,64,256]{3,2,1,0:T(8,128)(2,1)S(1)}, bf16[1,32,64,256]{3,2,1,0:T(8,128)(2,1)}, u32[]{:S(2)}) copy-start(bf16[1,32,64,256]{3,2,1,0:T(8,128)(2,1)} %param.12) | copy-start | bytes 3145732
  221.2 24.5 %all-to-all-start.7 = ((bf16[16,128,384]{2,0,1:T(8,128)(2,1)}), bf16[16,128,384]{2,0,1:T(8,128)(2,1)}, u32[]{:S(2)}, u32[]{:S(2)}) async-start(bf16[16,128,384]{2,0,1:T(8,128)(2,1)} %copy.98), calls=%async_computation.7 | async-start | bytes 3145728 | tf_op jit(solution)/shard_map/all_to_all | solution.py:17
  233.6 16.6 %copy-start.23 = (bf16[16,4,32,384]{3,0,1,2:T(8,128)(2,1)S(1)}, bf16[16,4,32,384]{3,0,1,2:T(8,128)(2,1)}, u32[]{:S(2)}) copy-start(bf16[16,4,32,384]{3,0,1,2:T(8,128)(2,1)} %copy-done.22) | copy-start | bytes 4718596
  245.8 24.5 %all-to-all-start.11 = ((bf16[64,32,384]{2,1,0:T(8,128)(2,1)}), bf16[64,32,384]{2,1,0:T(8,128)(2,1)}, u32[]{:S(2)}, u32[]{:S(2)}) async-start(bf16[64,32,384]{2,1,0:T(8,128)(2,1)} %copy.115), calls=%async_computation.11 | async-start | bytes 3145728 | tf_op jit(solution)/shard_map/all_to_all | solution.py:21
  261.1 25.6 %copy-start.28 = (bf16[4,16,32,384]{3,1,0,2:T(8,128)(2,1)}, bf16[4,16,32,384]{3,1,0,2:T(8,128)(2,1)S(1)}, u32[]{:S(2)}) copy-start(bf16[4,16,32,384]{3,1,0,2:T(8,128)(2,1)S(1)} %copy.100) | copy-start | bytes 4718596
  270.3 24.7 %all-to-all-start.2 = ((bf16[16,128,384]{2,0,1:T(8,128)(2,1)}), bf16[16,128,384]{2,0,1:T(8,128)(2,1)}, u32[]{:S(2)}, u32[]{:S(2)}) async-start(bf16[16,128,384]{2,0,1:T(8,128)(2,1)} %copy.82), calls=%async_computation.2 | async-start | bytes 3145728 | tf_op jit(solution)/shard_map/all_to_all | solution.py:17
  286.8 2.7 copy-start.2
  289.4 9.9 %copy-start.21 = (bf16[16,4,32,384]{3,0,1,2:T(8,128)(2,1)S(1)}, bf16[16,4,32,384]{3,0,1,2:T(8,128)(2,1)}, u32[]{:S(2)}) copy-start(bf16[16,4,32,384]{3,0,1,2:T(8,128)(2,1)} %copy-done.20) | copy-start | bytes 4718596
  294.9 31.5 %all-to-all-start.9 = ((bf16[64,32,384]{2,1,0:T(8,128)(2,1)}), bf16[64,32,384]{2,1,0:T(8,128)(2,1)}, u32[]{:S(2)}, u32[]{:S(2)}) async-start(bf16[64,32,384]{2,1,0:T(8,128)(2,1)} %copy.105), calls=%async_computation.9 | async-start | bytes 3145728 | tf_op jit(solution)/shard_map/all_to_all | solution.py:21
  304.6 72.6 %collective-permute-start.3 = (f32[2048,384]{1,0:T(8,128)}, f32[2048,384]{1,0:T(8,128)}, u32[]{:S(2)}, u32[]{:S(2)}) collective-permute-start(f32[2048,384]{1,0:T(8,128)} %get-tuple-element.25), channel_id=1, source_target_pairs={{0,24},{4,28},{8,0},{12,4},{16,8},{20,12},{24,16},{28,20},{1,25},{... | collective-permute-start | bytes 9437192 | tf_op jit(solution)/shard_map/ppermute | solution.py:9
  314.1 168.1 %collective-permute-start = (f32[2048,384]{1,0:T(8,128)}, f32[2048,384]{1,0:T(8,128)}, u32[]{:S(2)}, u32[]{:S(2)}) collective-permute-start(f32[2048,384]{1,0:T(8,128)} %get-tuple-element.27), channel_id=1, source_target_pairs={{0,8},{4,12},{8,16},{12,20},{16,24},{20,28},{24,0},{28,4},{1,9},{5... | collective-permute-start | bytes 9437192 | tf_op jit(solution)/shard_map/ppermute | solution.py:9
  322.9 8.2 %copy-start.7 = (bf16[1,1,2048,384]{3,2,1,0:T(8,128)(2,1)S(1)}, bf16[1,1,2048,384]{3,2,1,0:T(8,128)(2,1)}, u32[]{:S(2)}) copy-start(bf16[1,1,2048,384]{3,2,1,0:T(8,128)(2,1)} %copy-done.6) | copy-start | bytes 4718596
  326.5 24.7 %all-to-all-start.3 = ((bf16[64,32,384]{2,1,0:T(8,128)(2,1)}), bf16[64,32,384]{2,1,0:T(8,128)(2,1)}, u32[]{:S(2)}, u32[]{:S(2)}) async-start(bf16[64,32,384]{2,1,0:T(8,128)(2,1)} %copy.86), calls=%async_computation.3 | async-start | bytes 3145728 | tf_op jit(solution)/shard_map/all_to_all | solution.py:21
  331.1 3.3 copy-start.9
  331.1 3.3 copy-start.25
  334.4 1.4 copy-start.24
  342.4 10.6 %copy-start.18 = (bf16[1,16,128,128]{3,2,1,0:T(8,128)(2,1)S(1)}, bf16[1,16,128,128]{3,2,1,0:T(8,128)(2,1)}, u32[]{:S(2)}) copy-start(bf16[1,16,128,128]{3,2,1,0:T(8,128)(2,1)} %param.13) | copy-start | bytes 1572868
  342.4 135.5 %collective-permute-start.5 = (bf16[2048,384]{1,0:T(8,128)(2,1)}, bf16[2048,384]{1,0:T(8,128)(2,1)}, u32[]{:S(2)}, u32[]{:S(2)}) collective-permute-start(bf16[2048,384]{1,0:T(8,128)(2,1)} %bitcast.64), channel_id=1, source_target_pairs={{0,28},{4,0},{8,4},{12,8},{16,12},{20,16},{24,20},{28,24},{1,29},{... | collective-permute-start | bytes 4718600 | tf_op jit(solution)/shard_map/ppermute | solution.py:9
  351.2 3.7 copy-start.27
  351.2 3.7 copy-start.29
  353.0 11.4 %slice-start = ((s8[6291456]{0:T(1024)(128)(4,1)}), s8[4194304]{0:T(1024)(128)(4,1)S(1)}, s32[]{:S(2)}) async-start(s8[6291456]{0:T(1024)(128)(4,1)} %bitcast.260), calls=%async_computation.12 | async-start | bytes 8388608
  354.8 9.6 %slice-start.1 = ((s8[6291456]{0:T(1024)(128)(4,1)}), s8[2097152]{0:T(1024)(128)(4,1)S(1)}, s32[]{:S(2)}) async-start(s8[6291456]{0:T(1024)(128)(4,1)} %bitcast.260), calls=%async_computation.13 | async-start | bytes 4194304
  354.8 9.6 %copy-start.11 = (bf16[16,4,32,384]{3,0,1,2:T(8,128)(2,1)S(1)}, bf16[16,4,32,384]{3,0,1,2:T(8,128)(2,1)}, u32[]{:S(2)}) copy-start(bf16[16,4,32,384]{3,0,1,2:T(8,128)(2,1)} %copy-done.10) | copy-start | bytes 4718596
  354.8 9.6 %copy-start.19 = (f32[32,64,256]{2,1,0:T(8,128)S(1)}, f32[32,64,256]{2,1,0:T(8,128)}, u32[]{:S(2)}) copy-start(f32[32,64,256]{2,1,0:T(8,128)} %fusion.108) | copy-start | bytes 6291460
  354.8 127.4 %collective-permute-start.2 = (bf16[2048,384]{1,0:T(8,128)(2,1)}, bf16[2048,384]{1,0:T(8,128)(2,1)}, u32[]{:S(2)}, u32[]{:S(2)}) collective-permute-start(bf16[2048,384]{1,0:T(8,128)(2,1)} %bitcast.28), channel_id=1, source_target_pairs={{0,4},{4,8},{8,12},{12,16},{16,20},{20,24},{24,28},{28,0},{1,5},{5... | collective-permute-start | bytes 4718600 | tf_op jit(solution)/shard_map/ppermute | solution.py:9
  364.4 2.6 copy-start.5
  364.4 2.6 copy-start.26

commit v2 on v1

--- a/solution.py
+++ b/solution.py
@@ -79,35 +79,53 @@
     blocks = up_first.shape[0]
     width = up_first.shape[1]
     rows = activation.shape[1]
-    stored = stash[0, 0].reshape(blocks, width, rows)
+    far_activation = shifted(activation, "pipe", 2)
+    far_cotangent = shifted(cotangent, "pipe", -2)
+
     current = activation.astype(jnp.bfloat16).reshape(blocks, width, rows)
     folded_ahead = front(current, up_first, up_second, down_first)[3]
-    behind = front(stored, up_first, up_second, down_first)
-    output = activation + jnp.einsum(
-        "nir,nik->nkr", folded_ahead, down_second, preferred_element_type=jnp.float32
-    ).reshape(activation.shape)
-    grad_input, terms = backward(
-        stored, cotangent, up_first, up_second, down_first, down_second, behind
-    )
-    grad_input = cotangent + grad_input
-    totals = terms
-    near_activation = shifted(output.astype(jnp.bfloat16), "pipe", 1)
-    near_cotangent = shifted(grad_input.astype(jnp.bfloat16), "pipe", -1)
-    far_activation = shifted(output, "pipe", 2)
-    far_cotangent = shifted(grad_input, "pipe", -2)
-
-    stored = stash[1, 0].reshape(blocks, width, rows)
-    current = near_activation.reshape(blocks, width, rows)
-    folded_ahead = front(current, up_first, up_second, down_first)[3]
-    behind = front(stored, up_first, up_second, down_first)
     step = jnp.einsum(
         "nir,nik->nkr", folded_ahead, down_second, preferred_element_type=jnp.float32
     ).reshape(activation.shape)
+    output = activation + step
+    near_activation = shifted(output.astype(jnp.bfloat16), "pipe", 1)
+    step, cotangent = lax.optimization_barrier((step, cotangent))
+
+    stored = stash[0, 0].reshape(blocks, width, rows)
+    behind = front(stored, up_first, up_second, down_first)
+    grad_step, totals = backward(
+        stored, cotangent, up_first, up_second, down_first, down_second, behind
+    )
+    grad_input = cotangent + grad_step
+    near_cotangent = shifted(grad_input.astype(jnp.bfloat16), "pipe", -1)
+    step, grad_step, far_activation, far_cotangent = lax.optimization_barrier(
+        (step, grad_step, far_activation, far_cotangent)
+    )
+    far_step = shifted(step.astype(jnp.bfloat16), "pipe", 2)
+    far_grad_step = shifted(grad_step.astype(jnp.bfloat16), "pipe", -2)
+
+    current = near_activation.reshape(blocks, width, rows)
+    folded_ahead = front(current, up_first, up_second, down_first)[3]
+    step = jnp.einsum(
+        "nir,nik->nkr", folded_ahead, down_second, preferred_element_type=jnp.float32
+    ).reshape(activation.shape)
+    last_step = shifted(step.astype(jnp.bfloat16), "pipe", 1)
+    step, near_cotangent, far_step, far_grad_step = lax.optimization_barrier(
+        (step, near_cotangent, far_step, far_grad_step)
+    )
+
+    stored = stash[1, 0].reshape(blocks, width, rows)
+    behind = front(stored, up_first, up_second, down_first)
     grad_step, terms = backward(
         stored, near_cotangent, up_first, up_second, down_first, down_second, behind
     )
-    activation = far_activation + shifted(step.astype(jnp.bfloat16), "pipe", 1)
-    cotangent = far_cotangent + shifted(grad_step.astype(jnp.bfloat16), "pipe", -1)
+    last_grad_step = shifted(grad_step.astype(jnp.bfloat16), "pipe", -1)
+    activation = far_activation + (
+        far_step.astype(jnp.float32) + last_step.astype(jnp.float32)
+    )
+    cotangent = far_cotangent + (
+        far_grad_step.astype(jnp.float32) + last_grad_step.astype(jnp.float32)
+    )
     totals = (
         totals[0] + terms[0],
         totals[1] + terms[1],

time: 496 us -> 508 us (1.024)
  other arithmetic: 16.1 us -> 23 us
  waiting for transfers between devices: 222 us -> 228 us
    all_to_all x6, waiting for transfers between devices: 53.8 us -> 26.5 us  [to_columns(): lax.all_to_all(value, 'tensor', split_axis=1, concat_axis=0, tiled=True)]
    all_to_all x6, waiting for transfers between devices: 16.7 us -> 34.6 us  [to_rows(): lax.all_to_all(value, 'tensor', split_axis=0, concat_axis=1, tiled=True)]
    ppermute x6 -> x8, waiting for transfers between devices: 151 us -> 167 us  [shifted(): lax.ppermute(value, axis, [(i, (i + by) % count) for i in range(count)])]
    ppermute x6 -> x8, starting transfers between devices: 14.4 us -> 12.6 us  [shifted(): lax.ppermute(value, axis, [(i, (i + by) % count) for i in range(count)])]
  transfers between devices with their start and end apart: 18 -> 20, of which waited for: 12 -> 15; matrix products, arithmetic and copies ran while one was open for 37% -> 38% of each run, Pallas kernels for 0% -> 0%
where the time goes in v2:
time: 508 us; the launch traced here: 498 us
  waiting for transfers between devices  228 us (45%)
  matrix products  116 us (23%)
  starting transfers between devices  65.9 us (13%)
  local copies, waits for them, and re-layouts  63.2 us (12%)
  other arithmetic  23 us (5%)
    ppermute x8, waiting for transfers between devices, shifted(): lax.ppermute(value, axis, [(i, (i + by) % count) for i in range(count)])  167 us
    all_to_all x6, waiting for transfers between devices, to_rows(): lax.all_to_all(value, 'tensor', split_axis=0, concat_axis=1, tiled=True)  34.6 us
    all_to_all x6, starting transfers between devices, to_columns(): lax.all_to_all(value, 'tensor', split_axis=1, concat_axis=0, tiled=True)  26.8 us
    all_to_all x6, waiting for transfers between devices, to_columns(): lax.all_to_all(value, 'tensor', split_axis=1, concat_axis=0, tiled=True)  26.5 us
    all_to_all x6, starting transfers between devices, to_rows(): lax.all_to_all(value, 'tensor', split_axis=0, concat_axis=1, tiled=True)  26.5 us
    dot_general x4, matrix products, front(): jnp.einsum('ifr,inf->nir', hidden, first_down, preferred_element_type=jnp...  25.2 us
    dot_general x2, matrix products, backward(): jnp.einsum('nir,inf->ifr', grad_folded, first_down, preferred_element_typ...  24.4 us
    dot_general x2, matrix products, backward(): jnp.einsum('ifr,nir->inf', hidden, grad_folded, preferred_element_type=jn...  15.3 us
  transfers between devices with their start and end apart: 20, of which 15 were waited for; matrix products, arithmetic and copies ran while one was open for 38% of the time, Pallas kernels for 0%

profile of v2, /device:TPU:0, one launch (start us, length us, event | category | flops | bytes accessed | tf_op | source)
XLA Modules:
  0.0 497.8 jit_solution(13819847129199727905)
XLA Ops:
  0.7 2.2 convert_element_type.127
  3.5 2.1 copy.78
  5.5 4.4 all-to-all-start
  9.9 2.2 fusion.106
  13.9 2.1 copy.107
  16.0 14.7 %all-to-all-done = bf16[16,128,384]{2,0,1:T(8,128)(2,1)} async-done(((bf16[16,128,384]{2,0,1:T(8,128)(2,1)}), bf16[16,128,384]{2,0,1:T(8,128)(2,1)}, u32[]{:S(2)}, u32[]{:S(2)}) %all-to-all-start) | async-done | bytes 1572896 | tf_op jit(solution)/shard_map/all_to_all | solution.py:17
  30.6 4.3 all-to-all-start.8
  35.0 2.8 copy.79
  37.8 7.6 %fusion.55 = bf16[64,32,384]{2,0,1:T(8,128)(2,1)} fusion(bf16[64,32,384]{2,0,1:T(8,128)(2,1)} %bitcast.292, bf16[1,32,64,256]{3,2,1,0:T(8,128)(2,1)} %param.12, bf16[1,32,64,256]{3,2,1,0:T(8,128)(2,1)S(1)} %copy-done), kind=kOutput, calls=%fused_computation.74 | convolution fusion | flops 834404352 | bytes 5242880 | tf_op jit(solution)/shard_map/ifr,inf->nir/dot_general | solution.py:31
  45.5 3.5 copy.81
  48.9 6.2 %all-to-all-done.8 = bf16[16,128,384]{2,0,1:T(8,128)(2,1)} async-done(((bf16[16,128,384]{2,0,1:T(8,128)(2,1)}), bf16[16,128,384]{2,0,1:T(8,128)(2,1)}, u32[]{:S(2)}, u32[]{:S(2)}) %all-to-all-start.8) | async-done | bytes 1572896 | tf_op jit(solution)/shard_map/all_to_all | solution.py:17
  55.1 4.4 all-to-all-start.1
  60.1 2.1 copy.89
  62.2 17.4 %all-to-all-done.1 = bf16[64,32,384]{2,1,0:T(8,128)(2,1)} async-done(((bf16[64,32,384]{2,1,0:T(8,128)(2,1)}), bf16[64,32,384]{2,1,0:T(8,128)(2,1)}, u32[]{:S(2)}, u32[]{:S(2)}) %all-to-all-start.1) | async-done | bytes 1572896 | tf_op jit(solution)/shard_map/all_to_all | solution.py:21
  79.7 4.5 all-to-all-start.3
  84.2 4.5 collective-permute-start.1
  90.5 2.2 copy.82
  92.7 2.3 fusion.87
  98.4 2.9 copy.85
  101.3 3.0 all-to-all-done.3
  104.4 4.4 all-to-all-start.2
  108.7 6.4 %fusion.74 = f32[32,384,256]{2,1,0:T(8,128)} fusion(bf16[64,32,384]{2,0,1:T(8,128)(2,1)S(1)} %bitcast.273, bf16[1,32,64,256]{3,2,1,0:T(8,128)(2,1)S(1)} %copy-done), kind=kOutput, calls=%fused_computation.93 | convolution fusion | flops 402653184 | bytes 15204352 | tf_op jit(solution)/shard_map/nir,inf->ifr/dot_general | solution.py:29
  118.0 8.6 %fusion.34 = (bf16[32,256,384]{1,2,0:T(8,128)(2,1)}, f32[32,384,256]{2,1,0:T(8,128)}) fusion(bf16[64,32,384]{2,0,1:T(8,128)(2,1)S(1)} %bitcast.281, bf16[1,32,64,256]{3,2,1,0:T(8,128)(2,1)S(1)} %copy-done), kind=kOutput, calls=%fused_computation.45 | convolution fusion | flops 430964736 | bytes 21495808 | tf_op jit(solution)/shard_map/nir,inf->ifr/dot_general | solution.py:29
  126.6 2.3 all-to-all-done.2
  130.6 12.2 %fusion.6 = bf16[32,256,384]{1,2,0:T(8,128)(2,1)S(1)} fusion(f32[32,384,256]{2,1,0:T(8,128)} %get-tuple-element.45, bf16[64,32,384]{2,0,1:T(8,128)(2,1)S(1)} %bitcast.283, bf16[1,32,64,256]{3,2,1,0:T(8,128)(2,1)S(1)} %copy-done.28), kind=kOutput, calls=%fused_computation.12 | convolution fusion | flops 465567744 | bytes 21495808 | tf_op jit(solution)/shard_map/nir,inf->ifr/dot_general | solution.py:51
  145.4 2.1 copy.92
  147.4 4.6 all-to-all-start.4
  152.0 7.9 %fusion.61 = bf16[64,32,384]{2,0,1:T(8,128)(2,1)S(1)} fusion(bf16[1,32,64,256]{3,2,1,0:T(8,128)(2,1)S(1)} %copy-done.28, f32[32,384,256]{2,1,0:T(8,128)} %fusion.74), kind=kOutput, calls=%fused_computation.78 | convolution fusion | flops 431751168 | bytes 15204352 | tf_op jit(solution)/shard_map/ifr,inf->nir/dot_general | solution.py:31
  160.0 2.1 copy.120
  162.0 10.1 %all-to-all-done.4 = bf16[64,32,384]{2,1,0:T(8,128)(2,1)} async-done(((bf16[64,32,384]{2,1,0:T(8,128)(2,1)}), bf16[64,32,384]{2,1,0:T(8,128)(2,1)}, u32[]{:S(2)}, u32[]{:S(2)}) %all-to-all-start.4) | async-done | bytes 1572896 | tf_op jit(solution)/shard_map/all_to_all | solution.py:21
  172.1 4.3 all-to-all-start.11
  176.5 4.4 add_convert_fusion.1
  180.9 2.4 collective-permute-start.2
  185.4 2.1 copy.117
  189.8 35.5 %collective-permute-done = f32[2048,384]{1,0:T(8,128)} collective-permute-done((f32[2048,384]{1,0:T(8,128)}, f32[2048,384]{1,0:T(8,128)}, u32[]{:S(2)}, u32[]{:S(2)}) %collective-permute-start) | collective-permute-done | bytes 3145760 | tf_op jit(solution)/shard_map/ppermute | solution.py:9
  228.0 4.4 all-to-all-start.10
  232.3 4.3 add_convert_fusion
  236.6 3.5 collective-permute-start.3
  242.2 18.3 %collective-permute-done.2 = bf16[2048,384]{1,0:T(8,128)(2,1)} collective-permute-done((bf16[2048,384]{1,0:T(8,128)(2,1)}, bf16[2048,384]{1,0:T(8,128)(2,1)}, u32[]{:S(2)}, u32[]{:S(2)}) %collective-permute-start.2) | collective-permute-done | bytes 1572896 | tf_op jit(solution)/shard_map/ppermute | solution.py:9
  260.5 3.2 fusion.63
  263.7 2.9 copy.95
  266.6 4.4 all-to-all-start.5
  271.0 3.0 copy.121
  277.4 16.2 %collective-permute-done.3 = bf16[2048,384]{1,0:T(8,128)(2,1)} collective-permute-done((bf16[2048,384]{1,0:T(8,128)(2,1)}, bf16[2048,384]{1,0:T(8,128)(2,1)}, u32[]{:S(2)}, u32[]{:S(2)}) %collective-permute-start.3) | collective-permute-done | bytes 1572896 | tf_op jit(solution)/shard_map/ppermute | solution.py:9
  293.7 15.2 %collective-permute-done.5 = bf16[2048,384]{1,0:T(8,128)(2,1)} collective-permute-done((bf16[2048,384]{1,0:T(8,128)(2,1)}, bf16[2048,384]{1,0:T(8,128)(2,1)}, u32[]{:S(2)}, u32[]{:S(2)}) %collective-permute-start.5) | collective-permute-done | bytes 1572896 | tf_op jit(solution)/shard_map/ppermute | solution.py:9
  308.9 34.2 %collective-permute-done.4 = bf16[2048,384]{1,0:T(8,128)(2,1)} collective-permute-done((bf16[2048,384]{1,0:T(8,128)(2,1)}, bf16[2048,384]{1,0:T(8,128)(2,1)}, u32[]{:S(2)}, u32[]{:S(2)}) %collective-permute-start.4) | collective-permute-done | bytes 1572896 | tf_op jit(solution)/shard_map/ppermute | solution.py:9
  343.1 3.2 fusion.64
  346.3 2.9 copy.103
  349.2 4.8 all-to-all-start.7
  354.0 5.8 %fusion.109 = f32[32,64,256]{2,1,0:T(8,128)} fusion(bf16[64,32,384]{2,0,1:T(8,128)(2,1)} %bitcast.284, bf16[32,256,384]{1,2,0:T(8,128)(2,1)} %get-tuple-element.44), kind=kOutput, calls=%fused_computation.125 | convolution fusion | flops 402653184 | bytes 9961472 | tf_op jit(solution)/shard_map/ifr,nir->inf/dot_general | solution.py:48
  359.9 2.8 copy.97
  362.7 7.6 %fusion.52 = bf16[64,32,384]{2,0,1:T(8,128)(2,1)} fusion(bf16[64,32,384]{2,0,1:T(8,128)(2,1)} %bitcast.293, bf16[1,32,64,256]{3,2,1,0:T(8,128)(2,1)} %param.12, bf16[1,32,64,256]{3,2,1,0:T(8,128)(2,1)S(1)} %copy-done), kind=kOutput, calls=%fused_computation.73 | convolution fusion | flops 834404352 | bytes 5242880 | tf_op jit(solution)/shard_map/ifr,inf->nir/dot_general | solution.py:31
  370.3 3.5 copy.99
  374.1 4.5 all-to-all-start.6
  380.5 12.2 %fusion.13 = bf16[32,256,384]{1,2,0:T(8,128)(2,1)S(1)} fusion(f32[32,384,256]{2,1,0:T(8,128)} %fusion.74, bf16[64,32,384]{2,0,1:T(8,128)(2,1)S(1)} %bitcast.290, bf16[1,32,64,256]{3,2,1,0:T(8,128)(2,1)S(1)} %copy-done.30), kind=kOutput, calls=%fused_computation.19 | convolution fusion | flops 465567744 | bytes 21495808 | tf_op jit(solution)/shard_map/nir,inf->ifr/dot_general | solution.py:51
  398.8 4.3 all-to-all-start.9
  403.2 5.9 %fusion.108 = f32[32,64,256]{2,1,0:T(8,128)} fusion(bf16[64,32,384]{2,0,1:T(8,128)(2,1)} %bitcast.282, bf16[32,256,384]{1,2,0:T(8,128)(2,1)} %copy-done.3), kind=kOutput, calls=%fused_computation.124 | convolution fusion | flops 402653184 | bytes 9961472 | tf_op jit(solution)/shard_map/nir,ifr->inf/dot_general | solution.py:56
  410.9 3.2 fusion.65
  417.6 5.7 %all-to-all-done.9 = bf16[64,32,384]{2,1,0:T(8,128)(2,1)} async-done(((bf16[64,32,384]{2,1,0:T(8,128)(2,1)}), bf16[64,32,384]{2,1,0:T(8,128)(2,1)}, u32[]{:S(2)}, u32[]{:S(2)}) %all-to-all-start.9) | async-done | bytes 1572896 | tf_op jit(solution)/shard_map/all_to_all | solution.py:21
  427.1 9.5 %add_bitcast_fusion.2 = f32[1,32,64,256]{3,2,1,0:T(8,128)} fusion(f32[32,64,256]{2,1,0:T(8,128)S(1)} %copy-done.25, bf16[64,32,384]{2,0,1:T(8,128)(2,1)S(1)} %bitcast.291, f32[32,384,256]{2,1,0:T(8,128)} %fusion.74), kind=kOutput, calls=%fused_computation.58 | convolution fusion | flops 431489024 | bytes 18350080 | tf_op jit(solution)/shard_map/ifr,nir->inf/dot_general | solution.py:48
  436.6 2.6 add_bitcast_fusion.3
  439.2 47.0 %collective-permute-done.6 = bf16[2048,384]{1,0:T(8,128)(2,1)S(1)} collective-permute-done((bf16[2048,384]{1,0:T(8,128)(2,1)}, bf16[2048,384]{1,0:T(8,128)(2,1)S(1)}, u32[]{:S(2)}, u32[]{:S(2)}) %collective-permute-start.6) | collective-permute-done | bytes 1572896 | tf_op jit(solution)/shard_map/ppermute | solution.py:9
  486.1 4.4 add_bitcast_fusion.1
  492.7 4.9 add_bitcast_fusion
  (110 shorter events, 47.0 us)
Async XLA Ops:
  0.6 37.2 %copy-start = (bf16[1,32,64,256]{3,2,1,0:T(8,128)(2,1)S(1)}, bf16[1,32,64,256]{3,2,1,0:T(8,128)(2,1)}, u32[]{:S(2)}) copy-start(bf16[1,32,64,256]{3,2,1,0:T(8,128)(2,1)} %param.11) | copy-start | bytes 3145732
  0.6 2.2 copy-start.5
  5.5 25.1 %all-to-all-start = ((bf16[16,128,384]{2,0,1:T(8,128)(2,1)}), bf16[16,128,384]{2,0,1:T(8,128)(2,1)}, u32[]{:S(2)}, u32[]{:S(2)}) async-start(bf16[16,128,384]{2,0,1:T(8,128)(2,1)} %copy.78), calls=%async_computation | async-start | bytes 3145728 | tf_op jit(solution)/shard_map/all_to_all | solution.py:17
  12.1 1.1 copy-start.7
  12.1 47.4 %copy-start.9 = (bf16[1,1,2048,384]{3,2,1,0:T(8,128)(2,1)}, bf16[1,1,2048,384]{3,2,1,0:T(8,128)(2,1)S(1)}, u32[]{:S(2)}) copy-start(bf16[1,1,2048,384]{3,2,1,0:T(8,128)(2,1)S(1)} %get-tuple-element.43) | copy-start | bytes 4718596
  30.6 24.5 %all-to-all-start.8 = ((bf16[16,128,384]{2,0,1:T(8,128)(2,1)}), bf16[16,128,384]{2,0,1:T(8,128)(2,1)}, u32[]{:S(2)}, u32[]{:S(2)}) async-start(bf16[16,128,384]{2,0,1:T(8,128)(2,1)} %copy.107), calls=%async_computation.8 | async-start | bytes 3145728 | tf_op jit(solution)/shard_map/all_to_all | solution.py:17
  55.1 24.5 %all-to-all-start.1 = ((bf16[64,32,384]{2,1,0:T(8,128)(2,1)}), bf16[64,32,384]{2,1,0:T(8,128)(2,1)}, u32[]{:S(2)}, u32[]{:S(2)}) async-start(bf16[64,32,384]{2,1,0:T(8,128)(2,1)} %copy.81), calls=%async_computation.1 | async-start | bytes 3145728 | tf_op jit(solution)/shard_map/all_to_all | solution.py:21
  79.7 24.7 %all-to-all-start.3 = ((bf16[16,128,384]{2,0,1:T(8,128)(2,1)}), bf16[16,128,384]{2,0,1:T(8,128)(2,1)}, u32[]{:S(2)}, u32[]{:S(2)}) async-start(bf16[16,128,384]{2,0,1:T(8,128)(2,1)} %copy.89), calls=%async_computation.3 | async-start | bytes 3145728 | tf_op jit(solution)/shard_map/all_to_all | solution.py:17
  84.2 105.6 %collective-permute-start.1 = (f32[2048,384]{1,0:T(8,128)}, f32[2048,384]{1,0:T(8,128)}, u32[]{:S(2)}, u32[]{:S(2)}) collective-permute-start(f32[2048,384]{1,0:T(8,128)} %bitcast.278), channel_id=1, source_target_pairs={{0,24},{4,28},{8,0},{12,4},{16,8},{20,12},{24,16},{28,20},{1,25},{... | collective-permute-start | bytes 9437192 | tf_op jit(solution)/shard_map/ppermute | solution.py:9
  88.7 136.6 %collective-permute-start = (f32[2048,384]{1,0:T(8,128)}, f32[2048,384]{1,0:T(8,128)}, u32[]{:S(2)}, u32[]{:S(2)}) collective-permute-start(f32[2048,384]{1,0:T(8,128)} %bitcast.277), channel_id=1, source_target_pairs={{0,8},{4,12},{8,16},{12,20},{16,24},{20,28},{24,0},{28,4},{1,9},{5... | collective-permute-start | bytes 9437192 | tf_op jit(solution)/shard_map/ppermute | solution.py:9
  88.7 4.0 copy-start.16
  90.5 18.2 %copy-start.13 = (bf16[16,4,32,384]{3,0,1,2:T(8,128)(2,1)}, bf16[16,4,32,384]{3,0,1,2:T(8,128)(2,1)S(1)}, u32[]{:S(2)}) copy-start(bf16[16,4,32,384]{3,0,1,2:T(8,128)(2,1)S(1)} %copy.108) | copy-start | bytes 4718596
  92.7 2.6 copy-start.15
  95.5 1.1 copy-start.11
  104.4 24.5 %all-to-all-start.2 = ((bf16[16,128,384]{2,0,1:T(8,128)(2,1)}), bf16[16,128,384]{2,0,1:T(8,128)(2,1)}, u32[]{:S(2)}, u32[]{:S(2)}) async-start(bf16[16,128,384]{2,0,1:T(8,128)(2,1)} %copy.85), calls=%async_computation.2 | async-start | bytes 3145728 | tf_op jit(solution)/shard_map/all_to_all | solution.py:17
  116.8 1.2 copy-start.20
  126.6 4.0 copy-start.28
  130.5 12.2 %copy-start.21 = (bf16[4,16,32,384]{3,1,0,2:T(8,128)(2,1)}, bf16[4,16,32,384]{3,1,0,2:T(8,128)(2,1)S(1)}, u32[]{:S(2)}) copy-start(bf16[4,16,32,384]{3,1,0,2:T(8,128)(2,1)S(1)} %copy.87) | copy-start | bytes 4718596
  142.8 2.6 copy-start.3
  147.4 24.7 %all-to-all-start.4 = ((bf16[64,32,384]{2,1,0:T(8,128)(2,1)}), bf16[64,32,384]{2,1,0:T(8,128)(2,1)}, u32[]{:S(2)}, u32[]{:S(2)}) async-start(bf16[64,32,384]{2,1,0:T(8,128)(2,1)} %copy.92), calls=%async_computation.4 | async-start | bytes 3145728 | tf_op jit(solution)/shard_map/all_to_all | solution.py:21
  160.0 23.4 %slice-start = ((s8[6291456]{0:T(1024)(128)(4,1)}), s8[2097152]{0:T(1024)(128)(4,1)S(1)}, s32[]{:S(2)}) async-start(s8[6291456]{0:T(1024)(128)(4,1)} %bitcast.261), calls=%async_computation.12 | async-start | bytes 4194304
  172.1 55.8 %all-to-all-start.11 = ((bf16[64,32,384]{2,1,0:T(8,128)(2,1)}), bf16[64,32,384]{2,1,0:T(8,128)(2,1)}, u32[]{:S(2)}, u32[]{:S(2)}) async-start(bf16[64,32,384]{2,1,0:T(8,128)(2,1)} %copy.120), calls=%async_computation.11 | async-start | bytes 3145728 | tf_op jit(solution)/shard_map/all_to_all | solution.py:21
  176.5 6.8 %slice-start.1 = ((s8[6291456]{0:T(1024)(128)(4,1)}), s8[4194304]{0:T(1024)(128)(4,1)S(1)}, s32[]{:S(2)}) async-start(s8[6291456]{0:T(1024)(128)(4,1)} %bitcast.261), calls=%async_computation.13 | async-start | bytes 8388608
  176.5 6.8 %copy-start.29 = (bf16[1,32,64,256]{3,2,1,0:T(8,128)(2,1)S(1)}, bf16[1,32,64,256]{3,2,1,0:T(8,128)(2,1)}, u32[]{:S(2)}) copy-start(bf16[1,32,64,256]{3,2,1,0:T(8,128)(2,1)} %param.12) | copy-start | bytes 3145732
  180.9 79.5 %collective-permute-start.2 = (bf16[2048,384]{1,0:T(8,128)(2,1)}, bf16[2048,384]{1,0:T(8,128)(2,1)}, u32[]{:S(2)}, u32[]{:S(2)}) collective-permute-start(bf16[2048,384]{1,0:T(8,128)(2,1)} %add_convert_fusion.1), channel_id=1, source_target_pairs={{0,4},{4,8},{8,12},{12,16},{16,20},{20,24},{24,28},{28,0},{1,5},{5... | collective-permute-start | bytes 4718600 | tf_op jit(solution)/shard_map/ppermute | solution.py:9
  185.4 3.8 copy-start.6
  189.2 36.1 %copy-start.1 = (f32[16,384,128]{1,2,0:T(8,128)S(1)}, f32[16,384,128]{1,2,0:T(8,128)}, u32[]{:S(2)}) copy-start(f32[16,384,128]{1,2,0:T(8,128)} %fusion.87) | copy-start | bytes 9437188
  189.8 36.9 %copy-start.2 = (f32[16,384,128]{1,2,0:T(8,128)}, f32[16,384,128]{1,2,0:T(8,128)S(1)}, u32[]{:S(2)}) copy-start(f32[16,384,128]{1,2,0:T(8,128)S(1)} %fusion.89) | copy-start | bytes 9437188
  228.0 38.6 %all-to-all-start.10 = ((bf16[64,32,384]{2,1,0:T(8,128)(2,1)}), bf16[64,32,384]{2,1,0:T(8,128)(2,1)}, u32[]{:S(2)}, u32[]{:S(2)}) async-start(bf16[64,32,384]{2,1,0:T(8,128)(2,1)} %copy.117), calls=%async_computation.10 | async-start | bytes 3145728 | tf_op jit(solution)/shard_map/all_to_all | solution.py:21
  236.6 57.0 %collective-permute-start.3 = (bf16[2048,384]{1,0:T(8,128)(2,1)}, bf16[2048,384]{1,0:T(8,128)(2,1)}, u32[]{:S(2)}, u32[]{:S(2)}) collective-permute-start(bf16[2048,384]{1,0:T(8,128)(2,1)} %add_convert_fusion), channel_id=1, source_target_pairs={{0,28},{4,0},{8,4},{12,8},{16,12},{20,16},{24,20},{28,24},{1,29},{... | collective-permute-start | bytes 4718600 | tf_op jit(solution)/shard_map/ppermute | solution.py:9
  240.1 68.8 %collective-permute-start.5 = (bf16[2048,384]{1,0:T(8,128)(2,1)}, bf16[2048,384]{1,0:T(8,128)(2,1)}, u32[]{:S(2)}, u32[]{:S(2)}) collective-permute-start(bf16[2048,384]{1,0:T(8,128)(2,1)} %convert_element_type.148), channel_id=1, source_target_pairs={{0,24},{4,28},{8,0},{12,4},{16,8},{20,12},{24,16},{28,20},{1,25},{... | collective-permute-start | bytes 4718600 | tf_op jit(solution)/shard_map/ppermute | solution.py:9
  240.6 102.6 %collective-permute-start.4 = (bf16[2048,384]{1,0:T(8,128)(2,1)}, bf16[2048,384]{1,0:T(8,128)(2,1)}, u32[]{:S(2)}, u32[]{:S(2)}) collective-permute-start(bf16[2048,384]{1,0:T(8,128)(2,1)} %convert_element_type.147), channel_id=1, source_target_pairs={{0,8},{4,12},{8,16},{12,20},{16,24},{20,28},{24,0},{28,4},{1,9},{5... | collective-permute-start | bytes 4718600 | tf_op jit(solution)/shard_map/ppermute | solution.py:9
  266.6 82.7 %all-to-all-start.5 = ((bf16[16,128,384]{2,0,1:T(8,128)(2,1)}), bf16[16,128,384]{2,0,1:T(8,128)(2,1)}, u32[]{:S(2)}, u32[]{:S(2)}) async-start(bf16[16,128,384]{2,0,1:T(8,128)(2,1)} %copy.95), calls=%async_computation.5 | async-start | bytes 3145728 | tf_op jit(solution)/shard_map/all_to_all | solution.py:17
  271.0 4.7 copy-start.12
  274.0 69.2 %copy-start.17 = (bf16[1,16,128,128]{3,2,1,0:T(8,128)(2,1)S(1)}, bf16[1,16,128,128]{3,2,1,0:T(8,128)(2,1)}, u32[]{:S(2)}) copy-start(bf16[1,16,128,128]{3,2,1,0:T(8,128)(2,1)} %param.13) | copy-start | bytes 1572868
  349.2 24.9 %all-to-all-start.7 = ((bf16[16,128,384]{2,0,1:T(8,128)(2,1)}), bf16[16,128,384]{2,0,1:T(8,128)(2,1)}, u32[]{:S(2)}, u32[]{:S(2)}) async-start(bf16[16,128,384]{2,0,1:T(8,128)(2,1)} %copy.103), calls=%async_computation.7 | async-start | bytes 3145728 | tf_op jit(solution)/shard_map/all_to_all | solution.py:17
  374.1 24.7 %all-to-all-start.6 = ((bf16[64,32,384]{2,1,0:T(8,128)(2,1)}), bf16[64,32,384]{2,1,0:T(8,128)(2,1)}, u32[]{:S(2)}, u32[]{:S(2)}) async-start(bf16[64,32,384]{2,1,0:T(8,128)(2,1)} %copy.99), calls=%async_computation.6 | async-start | bytes 3145728 | tf_op jit(solution)/shard_map/all_to_all | solution.py:21
  378.7 1.8 copy-start.30
  380.5 12.2 %copy-start.26 = (bf16[4,16,32,384]{3,1,0,2:T(8,128)(2,1)}, bf16[4,16,32,384]{3,1,0,2:T(8,128)(2,1)S(1)}, u32[]{:S(2)}) copy-start(bf16[4,16,32,384]{3,1,0,2:T(8,128)(2,1)S(1)} %copy.105) | copy-start | bytes 4718596
  392.7 2.7 copy-start.4
  398.8 24.5 %all-to-all-start.9 = ((bf16[64,32,384]{2,1,0:T(8,128)(2,1)}), bf16[64,32,384]{2,1,0:T(8,128)(2,1)}, u32[]{:S(2)}, u32[]{:S(2)}) async-start(bf16[64,32,384]{2,1,0:T(8,128)(2,1)} %copy.110), calls=%async_computation.9 | async-start | bytes 3145728 | tf_op jit(solution)/shard_map/all_to_all | solution.py:21
  403.2 6.0 %copy-start.10 = (bf16[1,1,2048,384]{3,2,1,0:T(8,128)(2,1)S(1)}, bf16[1,1,2048,384]{3,2,1,0:T(8,128)(2,1)}, u32[]{:S(2)}) copy-start(bf16[1,1,2048,384]{3,2,1,0:T(8,128)(2,1)} %copy-done.9) | copy-start | bytes 4718596
  409.1 1.8 copy-start.22
  409.1 1.8 copy-start.23
  410.9 4.9 copy-start.18
  417.6 68.6 %collective-permute-start.6 = (bf16[2048,384]{1,0:T(8,128)(2,1)}, bf16[2048,384]{1,0:T(8,128)(2,1)S(1)}, u32[]{:S(2)}, u32[]{:S(2)}) collective-permute-start(bf16[2048,384]{1,0:T(8,128)(2,1)} %bitcast.222), channel_id=1, source_target_pairs={{0,4},{4,8},{8,12},{12,16},{16,20},{20,24},{24,28},{28,0},{1,5},{5... | collective-permute-start | bytes 4718600 | tf_op jit(solution)/shard_map/ppermute | solution.py:9
  423.3 3.8 copy-start.25
  423.3 3.8 copy-start.27
  425.1 11.5 %slice-start.2 = ((s8[6291456]{0:T(1024)(128)(4,1)}), s8[4194304]{0:T(1024)(128)(4,1)S(1)}, s32[]{:S(2)}) async-start(s8[6291456]{0:T(1024)(128)(4,1)} %bitcast.263), calls=%async_computation.14 | async-start | bytes 8388608
  426.9 9.7 %slice-start.3 = ((s8[6291456]{0:T(1024)(128)(4,1)}), s8[2097152]{0:T(1024)(128)(4,1)S(1)}, s32[]{:S(2)}) async-start(s8[6291456]{0:T(1024)(128)(4,1)} %bitcast.263), calls=%async_computation.15 | async-start | bytes 4194304
  426.9 9.7 %copy-start.14 = (bf16[16,4,32,384]{3,0,1,2:T(8,128)(2,1)S(1)}, bf16[16,4,32,384]{3,0,1,2:T(8,128)(2,1)}, u32[]{:S(2)}) copy-start(bf16[16,4,32,384]{3,0,1,2:T(8,128)(2,1)} %copy-done.13) | copy-start | bytes 4718596
  426.9 9.7 %copy-start.19 = (f32[32,64,256]{2,1,0:T(8,128)S(1)}, f32[32,64,256]{2,1,0:T(8,128)}, u32[]{:S(2)}) copy-start(f32[32,64,256]{2,1,0:T(8,128)} %fusion.108) | copy-start | bytes 6291460
  426.9 65.8 %collective-permute-start.7 = (bf16[2048,384]{1,0:T(8,128)(2,1)}, bf16[2048,384]{1,0:T(8,128)(2,1)}, u32[]{:S(2)}, u32[]{:S(2)}) collective-permute-start(bf16[2048,384]{1,0:T(8,128)(2,1)} %bitcast.69), channel_id=1, source_target_pairs={{0,28},{4,0},{8,4},{12,8},{16,12},{20,16},{24,20},{28,24},{1,29},{... | collective-permute-start | bytes 4718600 | tf_op jit(solution)/shard_map/ppermute | solution.py:9
  439.2 51.4 %copy-start.8 = (bf16[1,1,2048,384]{3,2,1,0:T(8,128)(2,1)S(1)}, bf16[1,1,2048,384]{3,2,1,0:T(8,128)(2,1)}, u32[]{:S(2)}) copy-start(bf16[1,1,2048,384]{3,2,1,0:T(8,128)(2,1)} %copy-done.7) | copy-start | bytes 4718596
  439.2 51.4 %copy-start.24 = (f32[16,128,128]{2,1,0:T(8,128)S(1)}, f32[16,128,128]{2,1,0:T(8,128)}, u32[]{:S(2)}) copy-start(f32[16,128,128]{2,1,0:T(8,128)} %fusion.107) | copy-start | bytes 3145732
